TPU v7x, 32 devices: a whole 2x2x4 slice. The times are simulated.
32 devices in a mesh: seq: 8 (over z, y), head: 2 (over x), cfg: 2 (over core).
Axes of the slice: x: 2, y: 2, z: 4, core: 2. Of those that a mesh axis runs over, the one named last changes fastest.
Arguments:
- queries: bfloat16 [6144, 5120], P(('cfg', 'seq'), 'head'), parts along dimension 0, may hold values from -16 to 16
- fresh_key: bfloat16 [6144, 5120], P(('cfg', 'seq'), 'head'), parts along dimension 0, may hold values from -16 to 16
- fresh_value: bfloat16 [6144, 5120], P(('cfg', 'seq'), 'head'), parts along dimension 0, may hold values from -6 to 6
- stale_key: bfloat16 [6144, 5120], P(('cfg', 'seq'), 'head'), parts along dimension 0, may hold values from -6 to 6
- stale_value: bfloat16 [6144, 5120], P(('cfg', 'seq'), 'head'), parts along dimension 0, may hold values from -6 to 6
- slot_tiles: int32 [48], P('cfg'), parts along dimension 0, may hold values from 0 to 23, as said below
- refresh: int32 [48], P('cfg'), parts along dimension 0, may hold values from 0 to 1, as said below
- stale_reads: int32 [16, 24], P('cfg'), parts along dimension 0, may hold values from 0 to 1, as said below
- out_weight: bfloat16 [5120, 5120], P('head'), may hold values from -6 to 6
Outputs:
- mixed: bfloat16 [6144, 5120], P(('cfg', 'seq', 'head')), parts along dimension 0
There are 2 independent parts, one for each index of `cfg`. A program takes and returns all parts, laid end to end along the dimension named above; an argument that names none is the same for every part. Nothing has to cross between parts.
Inputs may be any that keep to these rules, and one draw needn't show every extreme that they name: `slot_tiles`: A permutation of the 24 tiles. Cache slot i lies on index i // 3 of seq; the slots of every index of seq hold at least one tile that is not refreshed. `refresh`: tile t belongs to index t // 3 of seq. Every index of seq owns between 1 and 2 refreshed tiles; some index owns exactly 1 and some exactly 2. `stale_reads`: only tiles that are not refreshed are read. A reader reads at most one tile among the slots of any one index of seq; some reader reads one tile from the slots of every index.
All inputs are finite; a program needn't handle non-finite values.
Results may differ from a plain program's by a relative error of at most 0.019.
Values may be sent and summed in bfloat16 or wider, within the bound.
No kernel may reach another device: no remote copies, remote signals or barrier semaphores. Data moves between devices by JAX's collectives and lax.ppermute only.
A program may use at most 256 MiB of HBM per device.

v0:
```python
import jax
import jax.numpy as jnp
from jax import lax
from jax.sharding import PartitionSpec as P

HD = 128
TILE = 128


NEG = -1e30


def attend(carry, query3, keys, values, mask):
    count = keys.shape[0]
    heads_here = query3.shape[1]
    keys3 = keys.reshape(count, heads_here, HD)
    values3 = values.reshape(count, heads_here, HD)
    score = jnp.einsum("qhd,khd->qhk", query3, keys3, preferred_element_type=jnp.float32) * HD ** (
        -0.5
    )
    score = jnp.where(mask[None, None, :] > 0, score, NEG)
    top_old, total_old, summed_old = carry
    top_new = jnp.maximum(top_old, jnp.max(score, axis=2))
    weight = jnp.exp(score - top_new[:, :, None]) * mask[None, None, :]
    factor = jnp.exp(top_old - top_new)
    total_new = total_old * factor + jnp.sum(weight, axis=2)
    summed_new = summed_old * factor[:, :, None] + jnp.einsum(
        "qhk,khd->qhd", weight.astype(jnp.bfloat16), values3, preferred_element_type=jnp.float32
    )
    return (top_new, total_new, summed_new)


def on_device(
    queries,
    fresh_key,
    fresh_value,
    stale_key,
    stale_value,
    slot_tiles,
    refresh,
    stale_reads,
    out_weight,
):
    tokens_here = queries.shape[0]
    heads_here = queries.shape[1] // HD
    tile_dev = tokens_here // TILE
    total_tiles = refresh.shape[0]
    readers = stale_reads.shape[0]
    width_here = queries.shape[1]
    me = lax.axis_index("seq")
    query3 = queries.reshape(tokens_here, heads_here, HD)
    tile_ids = jnp.arange(total_tiles, dtype=jnp.int32)
    empty = (
        jnp.full((tokens_here, heads_here), NEG, jnp.float32),
        jnp.zeros((tokens_here, heads_here), jnp.float32),
        jnp.zeros((tokens_here, heads_here, HD), jnp.float32),
    )
    my_reads = lax.dynamic_slice_in_dim(stale_reads, me, 1, 0)[0]
    slot_match = (slot_tiles[:, None] == tile_ids[None, :]).astype(jnp.int32)
    slot_flags = jnp.sum(slot_match * my_reads[None, :], axis=1)
    holder_valid = jnp.sum(slot_flags.reshape(readers, tile_dev), axis=1)
    stale_mask = jnp.repeat(holder_valid, TILE).astype(jnp.float32)
    my_tiles = lax.dynamic_slice_in_dim(slot_tiles, me * tile_dev, tile_dev, 0)
    own_match = (my_tiles[:, None] == tile_ids[None, :]).astype(jnp.int32)
    wanted = jnp.sum(stale_reads[:, None, :] * own_match[None, :, :], axis=2).astype(jnp.bfloat16)
    send_key = jnp.einsum(
        "sj,jrf->srf",
        wanted,
        stale_key.reshape(tile_dev, TILE, width_here),
        preferred_element_type=jnp.float32,
    ).astype(jnp.bfloat16)
    send_value = jnp.einsum(
        "sj,jrf->srf",
        wanted,
        stale_value.reshape(tile_dev, TILE, width_here),
        preferred_element_type=jnp.float32,
    ).astype(jnp.bfloat16)
    got_key, got_value = (
        lax.all_to_all(send_key, "seq", split_axis=0, concat_axis=0, tiled=True),
        lax.all_to_all(send_value, "seq", split_axis=0, concat_axis=0, tiled=True),
    )
    got_key = got_key.reshape(readers * TILE, width_here)
    got_value = got_value.reshape(readers * TILE, width_here)
    start_carry = attend(empty, query3, got_key, got_value, stale_mask)
    pieces = (
        lax.all_gather(fresh_key, "seq", axis=0, tiled=True),
        lax.all_gather(fresh_value, "seq", axis=0, tiled=True),
    )
    count = pieces[0].shape[0]
    row_tiles = jnp.arange(count, dtype=jnp.int32) // TILE
    flags = jnp.sum(
        (row_tiles[:, None] == tile_ids[None, :]).astype(jnp.int32) * refresh[None, :], axis=1
    )
    folded = attend(start_carry, query3, pieces[0], pieces[1], flags.astype(jnp.float32))
    attended = (
        (folded[2] / folded[1][:, :, None]).reshape(tokens_here, width_here).astype(jnp.bfloat16)
    )
    return lax.psum_scatter(
        jnp.dot(attended, out_weight, preferred_element_type=jnp.float32).astype(jnp.bfloat16),
        "head",
        scatter_dimension=0,
        tiled=True,
    )


def solution(mesh):
    return jax.shard_map(
        on_device,
        mesh=mesh,
        in_specs=(
            P(("cfg", "seq"), "head"),
            P(("cfg", "seq"), "head"),
            P(("cfg", "seq"), "head"),
            P(("cfg", "seq"), "head"),
            P(("cfg", "seq"), "head"),
            P("cfg"),
            P("cfg"),
            P("cfg", None),
            P("head", None),
        ),
        out_specs=P(("cfg", "seq", "head"), None),
        check_vma=False,
    )
```

profile of v0, /device:TPU:0, one launch (start us, length us, event | category | flops | bytes accessed | tf_op | source)
XLA Modules:
  0.0 824.1 jit_solution(2785188553490503801)
XLA Ops:
  6.5 4.1 copy.55
  10.7 0.7 dynamic_slice.7
  11.4 0.1 fusion.27
  11.5 0.8 multiply_reduce_fusion
  12.3 2.4 convolution_convert_fusion.2
  14.7 3.8 copy.46
  18.5 7.3 all-to-all-start
  25.9 0.7 all-gather.5.cloned.1.call-update
  26.6 2.4 convolution_convert_fusion.1
  29.0 3.9 copy.52
  32.8 202.2 %all-to-all-done = bf16[8,128,2560]{2,1,0:T(8,128)(2,1)} async-done(((bf16[8,128,2560]{2,1,0:T(8,128)(2,1)}), bf16[8,128,2560]{2,1,0:T(8,128)(2,1)}, u32[]{:S(2)}, u32[]{:S(2)}) %all-to-all-start) | async-done | bytes 5242912 | tf_op jit(solution)/shard_map/all_to_all | solution.py:79
  235.0 4.6 all-to-all-start.1
  239.7 0.2 reduce-scatter.2.cloned.1.call-start
  239.9 2.8 copy.48
  242.7 0.1 select_reduce_fusion
  242.9 0.7 dynamic-slice_bitcast_fusion
  243.6 0.2 select_reduce_fusion.1
  243.8 0.1 reshape.104
  243.8 0.1 reduce_sum.55
  244.1 10.0 %reshape.111 = bf16[1024,20,128]{2,1,0:T(8,128)(2,1)} reshape(bf16[8,128,2560]{2,1,0:T(8,128)(2,1)} %all-to-all-done) | data formatting | bytes 10485760 | tf_op jit(solution)/shard_map/reshape;reshape | solution.py:16
  254.1 188.1 %all-to-all-done.1 = bf16[8,128,2560]{2,1,0:T(8,128)(2,1)} async-done(((bf16[8,128,2560]{2,1,0:T(8,128)(2,1)}), bf16[8,128,2560]{2,1,0:T(8,128)(2,1)}, u32[]{:S(2)}, u32[]{:S(2)}) %all-to-all-start.1) | async-done | bytes 5242912 | tf_op jit(solution)/shard_map/all_to_all | solution.py:80
  442.1 10.2 %reshape.112 = bf16[1024,20,128]{2,1,0:T(8,128)(2,1)} reshape(bf16[8,128,2560]{2,1,0:T(8,128)(2,1)} %all-to-all-done.1) | data formatting | bytes 10485760 | tf_op jit(solution)/shard_map/reshape;reshape | solution.py:17
  452.3 15.2 %bitcast_reduce_fusion.1 = (f32[384,20]{0,1:T(8,128)S(1)}, f32[20,1024,384]{2,1,0:T(8,128)}) fusion(pred[1024]{0:T(1024)(128)(4,1)S(1)} %bitcast_compare_fusion, bf16[384,20,128]{0,2,1:T(8,128)(2,1)S(1)} %bitcast.63, bf16[1024,20,128]{2,1,0:T(8,128)(2,1)} %reshape.111), kind=kOutput, calls=%fused_computation.9 | convolution fusion | flops 2036851200 | bytes 38697984 | tf_op jit(solution)/shard_map/qhd,khd->qhk/dot_general | solution.py:18
  467.5 41.6 %bitcast_reduce_fusion = (f32[384,20]{0,1:T(8,128)S(1)}, f32[20,3072,384]{2,1,0:T(8,128)}) fusion(pred[3072]{0:T(1024)(128)(4,1)S(1)} %broadcast_compare_fusion, bf16[3072,20,128]{0,2,1:T(8,128)(2,1)} %bitcast.61, bf16[384,20,128]{0,2,1:T(8,128)(2,1)S(1)} %bitcast.64), kind=kOutput, calls=%fused_computation.1 | convolution fusion | flops 6110568960 | bytes 112100352 | tf_op jit(solution)/shard_map/qhd,khd->qhk/dot_general | solution.py:18
  509.2 32.3 %fusion.2 = f32[384,20]{0,1:T(8,128)S(1)} fusion(f32[20,3072,384]{2,1,0:T(8,128)} %get-tuple-element.13, f32[3072]{0:T(1024)S(1)} %convert_element_type.64, f32[384,20]{0,1:T(8,128)S(1)} %get-tuple-element.8, pred[3072]{0:T(1024)(128)(4,1)S(1)} %broadcast_compare_fusion), kind=kLoop, calls=%fused_computation.5 | loop fusion | flops 117957120 | bytes 94448640 | tf_op jit(solution)/shard_map/reduce_sum | solution.py:26
  541.5 111.6 %all-gather.5.cloned.1.call-done = bf16[3072,2560]{1,0:T(8,128)(2,1)} async-done(((bf16[384,2560]{1,0:T(8,128)(2,1)}), bf16[3072,2560]{1,0:T(8,128)(2,1)}) %all-gather.5.cloned.1.call-update) | async-done | bytes 15728656 | tf_op jit(solution)/shard_map/all_gather | solution.py:87
  653.1 20.7 %copy.58 = bf16[3072,2560]{0,1:T(8,128)(2,1)} copy(bf16[3072,2560]{1,0:T(8,128)(2,1)} %all-gather.5.cloned.1.call-done) | data formatting | bytes 31457280 | tf_op jit(solution)/shard_map/all_gather | solution.py:87
  673.8 41.7 %fusion.4 = f32[20,384,128]{1,2,0:T(8,128)} fusion(bf16[3072,20,128]{0,2,1:T(8,128)(2,1)} %bitcast.62, f32[20,3072,384]{2,1,0:T(8,128)} %get-tuple-element.13, f32[3072]{0:T(1024)S(1)} %convert_element_type.64, f32[384,20]{0,1:T(8,128)S(1)} %get-tuple-element.8, pred[3072]{0:T(1024)(128)(4,1)S(1)} %broadcast_compare_fusion), kind=kOutput, calls=%fused_computation.7 | convolution fusion | flops 6157762560 | bytes 114078720 | tf_op jit(solution)/shard_map/qhk,khd->qhd/dot_general | solution.py:27
  715.5 14.5 %fusion.8 = f32[384,20]{0,1:T(8,128)S(1)} fusion(f32[20,1024,384]{2,1,0:T(8,128)} %get-tuple-element.11, f32[1024]{0:T(1024)S(1)} %broadcast_bitcast_fusion, f32[384,20]{0,1:T(8,128)S(1)} %get-tuple-element.9, pred[1024]{0:T(1024)(128)(4,1)S(1)} %bitcast_compare_fusion), kind=kLoop, calls=%fused_computation.13 | loop fusion | flops 39313920 | bytes 31523840 | tf_op jit(solution)/shard_map/reduce_sum | solution.py:26
  730.0 19.7 %fusion.16 = bf16[384,20,128]{0,2,1:T(8,128)(2,1)} fusion(f32[20,384,128]{1,2,0:T(8,128)} %fusion.4, f32[20,1024,384]{2,1,0:T(8,128)} %get-tuple-element.11, f32[1024]{0:T(1024)S(1)} %broadcast_bitcast_fusion, f32[384,20]{0,1:T(8,128)S(1)} %get-tuple-element.9, pred[1024]{0:T(1024)(128)(4,1)S(1)} %bitcast_compare_fusion, ...), kind=kOutput, calls=%fused_computation.24 | convolution fusion | flops 2057502720 | bytes 42726400 | tf_op jit(solution)/shard_map/qhk,khd->qhd/dot_general | solution.py:27
  749.7 17.4 %convolution_convert_fusion = bf16[384,5120]{1,0:T(8,128)(2,1)} fusion(bf16[384,2560]{0,1:T(8,128)(2,1)} %bitcast.66, bf16[2560,5120]{1,0:T(8,128)(2,1)} %param.17), kind=kOutput, calls=%fused_computation.16 | convolution fusion | flops 10068295680 | bytes 32112640 | tf_op jit(solution)/shard_map/dot_general | solution.py:99
  767.1 50.4 %reduce-scatter.2.cloned.1.call-done = bf16[192,5120]{1,0:T(8,128)(2,1)} async-done(((bf16[384,5120]{1,0:T(8,128)(2,1)}), bf16[192,5120]{1,0:T(8,128)(2,1)}) %reduce-scatter.2.cloned.1.call-update) | async-done | bytes 1966096 | tf_op jit(solution)/shard_map/reduce_scatter | solution.py:98
  (23 shorter events, 0.3 us)
Async XLA Ops:
  6.5 5.8 copy-start
  6.5 461.0 %all-gather.3.cloned.1.call-start = ((), (), s32[]{:S(2)}) async-start(), calls=%async_computation.3 | async-start | bytes 17694720 | tf_op jit(solution)/shard_map/all_gather | solution.py:86
  14.7 11.9 %copy-start.2 = (bf16[384,2560]{1,0:T(8,128)(2,1)S(1)}, bf16[384,2560]{1,0:T(8,128)(2,1)}, u32[]{:S(2)}) copy-start(bf16[384,2560]{1,0:T(8,128)(2,1)} %param.13) | copy-start | bytes 5898244
  18.5 216.5 %all-to-all-start = ((bf16[8,128,2560]{2,1,0:T(8,128)(2,1)}), bf16[8,128,2560]{2,1,0:T(8,128)(2,1)}, u32[]{:S(2)}, u32[]{:S(2)}) async-start(bf16[8,128,2560]{2,1,0:T(8,128)(2,1)} %copy.46), calls=%async_computation | async-start | bytes 10485760 | tf_op jit(solution)/shard_map/all_to_all | solution.py:79
  25.8 627.3 %all-gather.5.cloned.1.call-start = ((), (), s32[]{:S(2)}) async-start(), calls=%async_computation.4 | async-start | bytes 17694720 | tf_op jit(solution)/shard_map/all_gather | solution.py:87
  26.6 216.2 %copy-start.3 = (s32[24]{0:T(128)S(1)}, s32[24]{0:T(128)}, u32[]{:S(2)}) copy-start(s32[24]{0:T(128)} %param.15) | copy-start | bytes 292
  26.6 217.0 %copy-start.4 = (s32[24]{0:T(128)S(1)}, s32[24]{0:T(128)}, u32[]{:S(2)}) copy-start(s32[24]{0:T(128)} %param.14) | copy-start | bytes 292
  235.0 207.1 %all-to-all-start.1 = ((bf16[8,128,2560]{2,1,0:T(8,128)(2,1)}), bf16[8,128,2560]{2,1,0:T(8,128)(2,1)}, u32[]{:S(2)}, u32[]{:S(2)}) async-start(bf16[8,128,2560]{2,1,0:T(8,128)(2,1)} %copy.52), calls=%async_computation.1 | async-start | bytes 10485760 | tf_op jit(solution)/shard_map/all_to_all | solution.py:80
  239.7 577.9 %reduce-scatter.2.cloned.1.call-start = ((), (), s32[]{:S(2)}) async-start(), calls=%async_computation.5 | async-start | bytes 5898240 | tf_op jit(solution)/shard_map/reduce_scatter | solution.py:98
  749.7 67.8 %copy-start.1 = (bf16[384,2560]{1,0:T(8,128)(2,1)S(1)}, bf16[384,2560]{1,0:T(8,128)(2,1)}, u32[]{:S(2)}) copy-start(bf16[384,2560]{1,0:T(8,128)(2,1)} %param.12) | copy-start | bytes 5898244
Sparse Core Ops, SparseCore 0:
  10.8 426.9 all-gather.2
  439.9 213.1 all-gather.4
  767.3 50.2 reduce-scatter.1
where the time goes:
time: 826 us; the launch traced here: 824 us
  waiting for transfers between devices  553 us (67%)
  matrix products  140 us (17%)
  local copies, waits for them, and re-layouts  57 us (7%)
  other arithmetic  48.3 us (6%)
  between operations  13.3 us (2%)
  starting transfers between devices  12.2 us (1%)
    all_to_all x1, waiting for transfers between devices, on_device(): lax.all_to_all(send_key, 'seq', split_axis=0, concat_axis=0, tiled=True)  202 us
    all_to_all x1, waiting for transfers between devices, on_device(): lax.all_to_all(send_value, 'seq', split_axis=0, concat_axis=0, tiled=True)  188 us
    all_gather x1, waiting for transfers between devices, on_device(): lax.all_gather(fresh_value, 'seq', axis=0, tiled=True)  112 us
    dot_general x2, matrix products, attend(): jnp.einsum('qhk,khd->qhd', weight.astype(jnp.bfloat16), values3, preferre...  61.4 us
    dot_general x2, matrix products, attend(): jnp.einsum('qhd,khd->qhk', query3, keys3, preferred_element_type=jnp.floa...  56.8 us
    reduce_scatter x1, waiting for transfers between devices, on_device(): lax.psum_scatter(jnp.dot(attended, out_weight, preferred_element_type=jnp...  50.4 us
    reduce_sum x2, other arithmetic, attend(): total_new = total_old * factor + jnp.sum(weight, axis=2)  46.9 us
    all_gather x1, local copies, waits for them, and re-layouts, on_device(): lax.all_gather(fresh_value, 'seq', axis=0, tiled=True)  20.7 us
  transfers between devices with their start and end apart: 5, of which 4 were waited for; matrix products, arithmetic and copies ran while one was open for 15% of the time, Pallas kernels for 0%

commit v1 on v0

v1 whole, which is shorter than its diff:
```python
import jax
import jax.numpy as jnp
from jax import lax
from jax.experimental import pallas as pl
from jax.experimental.pallas import tpu as pltpu
from jax.sharding import PartitionSpec as P

HD = 128
TILE = 128


NEG = -1e30


def _scores(q_ref, kf0_ref, kf1_ref, ks_ref, j, second, valid):
    sl = slice(j * HD, (j + 1) * HD)
    qj = q_ref[0, :, sl]
    dims = (((1,), (1,)), ((), ()))
    scale = HD ** -0.5
    s0 = lax.dot_general(qj, kf0_ref[0, :, sl], dims, preferred_element_type=jnp.float32) * scale
    s1 = lax.dot_general(qj, kf1_ref[0, :, sl], dims, preferred_element_type=jnp.float32) * scale
    s2 = lax.dot_general(qj, ks_ref[0, :, sl], dims, preferred_element_type=jnp.float32) * scale
    s1 = jnp.where(second > 0, s1, NEG)
    s2 = jnp.where(valid > 0, s2, NEG)
    return s0, s1, s2


def max_kernel(fsel_ref, sidx_ref, sval_ref, q_ref, kf0_ref, kf1_ref, ks_ref, m_ref):
    r = pl.program_id(0)
    heads_here = q_ref.shape[2] // HD
    second = fsel_ref[2]
    valid = sval_ref[r]
    for j in range(heads_here):
        s0, s1, s2 = _scores(q_ref, kf0_ref, kf1_ref, ks_ref, j, second, valid)
        m = jnp.maximum(
            jnp.maximum(jnp.max(s0, axis=1, keepdims=True), jnp.max(s1, axis=1, keepdims=True)),
            jnp.max(s2, axis=1, keepdims=True),
        )
        m_ref[0, :, j : j + 1] = m


def acc_kernel(
    fsel_ref, sidx_ref, sval_ref, q_ref, kf0_ref, kf1_ref, ks_ref, vf0_ref, vf1_ref, vs_ref, m_ref,
    acc_ref, l_ref,
):
    r = pl.program_id(0)
    heads_here = q_ref.shape[2] // HD
    second = fsel_ref[2]
    valid = sval_ref[r]
    for j in range(heads_here):
        sl = slice(j * HD, (j + 1) * HD)
        s0, s1, s2 = _scores(q_ref, kf0_ref, kf1_ref, ks_ref, j, second, valid)
        top = m_ref[0, :, j : j + 1]
        w0 = jnp.exp(s0 - top)
        w1 = jnp.exp(s1 - top)
        w2 = jnp.exp(s2 - top)
        total = (
            jnp.sum(w0, axis=1, keepdims=True)
            + jnp.sum(w1, axis=1, keepdims=True)
            + jnp.sum(w2, axis=1, keepdims=True)
        )
        summed = (
            jnp.dot(w0.astype(jnp.bfloat16), vf0_ref[0, :, sl], preferred_element_type=jnp.float32)
            + jnp.dot(w1.astype(jnp.bfloat16), vf1_ref[0, :, sl], preferred_element_type=jnp.float32)
            + jnp.dot(w2.astype(jnp.bfloat16), vs_ref[0, :, sl], preferred_element_type=jnp.float32)
        )
        acc_ref[0, :, sl] = summed.astype(acc_ref.dtype)
        l_ref[0, :, j : j + 1] = total


def on_device(
    queries,
    fresh_key,
    fresh_value,
    stale_key,
    stale_value,
    slot_tiles,
    refresh,
    stale_reads,
    out_weight,
):
    tokens_here = queries.shape[0]
    width_here = queries.shape[1]
    heads_here = width_here // HD
    tile_dev = tokens_here // TILE
    readers = stale_reads.shape[0]
    me = lax.axis_index("seq")

    my_refresh = lax.dynamic_slice_in_dim(refresh, me * tile_dev, tile_dev, 0)
    first = jnp.argmax(my_refresh).astype(jnp.int32)
    last = (tile_dev - 1 - jnp.argmax(my_refresh[::-1])).astype(jnp.int32)
    second = (jnp.sum(my_refresh) >= 2).astype(jnp.int32)
    fsel = jnp.stack([first, last, second])

    my_slots = lax.dynamic_slice_in_dim(slot_tiles, me * tile_dev, tile_dev, 0)
    wanted = jnp.take(stale_reads, my_slots, axis=1)
    sidx = jnp.argmax(wanted, axis=1).astype(jnp.int32)
    sval = jnp.max(wanted, axis=1).astype(jnp.int32)

    q_all = lax.all_gather(queries, "seq", axis=0, tiled=False)
    fk3 = fresh_key.reshape(tile_dev, TILE, width_here)
    fv3 = fresh_value.reshape(tile_dev, TILE, width_here)
    sk3 = stale_key.reshape(tile_dev, TILE, width_here)
    sv3 = stale_value.reshape(tile_dev, TILE, width_here)

    q_spec = pl.BlockSpec((1, tokens_here, width_here), lambda r, f, s, v: (r, 0, 0))
    f0_spec = pl.BlockSpec((1, TILE, width_here), lambda r, f, s, v: (f[0], 0, 0))
    f1_spec = pl.BlockSpec((1, TILE, width_here), lambda r, f, s, v: (f[1], 0, 0))
    s_spec = pl.BlockSpec((1, TILE, width_here), lambda r, f, s, v: (s[r], 0, 0))
    stat_spec = pl.BlockSpec((1, tokens_here, heads_here), lambda r, f, s, v: (r, 0, 0))
    stat_shape = jax.ShapeDtypeStruct((readers, tokens_here, heads_here), jnp.float32)
    params = pltpu.CompilerParams(dimension_semantics=("arbitrary",))

    local_top = pl.pallas_call(
        max_kernel,
        grid_spec=pltpu.PrefetchScalarGridSpec(
            num_scalar_prefetch=3,
            grid=(readers,),
            in_specs=[q_spec, f0_spec, f1_spec, s_spec],
            out_specs=stat_spec,
        ),
        out_shape=stat_shape,
        compiler_params=params,
    )(fsel, sidx, sval, q_all, fk3, fk3, sk3)
    top = lax.pmax(local_top, "seq")

    summed, total = pl.pallas_call(
        acc_kernel,
        grid_spec=pltpu.PrefetchScalarGridSpec(
            num_scalar_prefetch=3,
            grid=(readers,),
            in_specs=[q_spec, f0_spec, f1_spec, s_spec, f0_spec, f1_spec, s_spec, stat_spec],
            out_specs=[q_spec, stat_spec],
        ),
        out_shape=[
            jax.ShapeDtypeStruct((readers, tokens_here, width_here), jnp.bfloat16),
            stat_shape,
        ],
        compiler_params=params,
    )(fsel, sidx, sval, q_all, fk3, fk3, sk3, fv3, fv3, sv3, top)

    summed = lax.psum_scatter(summed, "seq", scatter_dimension=0, tiled=True)[0]
    total = lax.psum_scatter(total, "seq", scatter_dimension=0, tiled=True)[0]
    attended = (
        (summed.astype(jnp.float32).reshape(tokens_here, heads_here, HD) / total[:, :, None])
        .reshape(tokens_here, width_here)
        .astype(jnp.bfloat16)
    )
    return lax.psum_scatter(
        jnp.dot(attended, out_weight, preferred_element_type=jnp.float32).astype(jnp.bfloat16),
        "head",
        scatter_dimension=0,
        tiled=True,
    )


def solution(mesh):
    return jax.shard_map(
        on_device,
        mesh=mesh,
        in_specs=(
            P(("cfg", "seq"), "head"),
            P(("cfg", "seq"), "head"),
            P(("cfg", "seq"), "head"),
            P(("cfg", "seq"), "head"),
            P(("cfg", "seq"), "head"),
            P("cfg"),
            P("cfg"),
            P("cfg", None),
            P("head", None),
        ),
        out_specs=P(("cfg", "seq", "head"), None),
        check_vma=False,
    )
```

time: 826 us -> 798 us (0.966)
  matrix products: 140 us -> 18.4 us
  waiting for transfers between devices: 553 us -> 660 us
  Pallas kernels: 0 us -> 88.3 us
  local copies, waits for them, and re-layouts: 57 us -> 10.1 us
  other arithmetic: 48.3 us -> 5.96 us
  starting transfers between devices: 12.2 us -> 0.34 us
    all_to_all x2 -> x0, waiting for transfers between devices: 390 us -> none  [the longest x1 202 us: on_device(): lax.all_to_all(send_key, 'seq', split_axis=0, concat_axis=0, tiled=True)]
    reduce_scatter x0 -> x2, waiting for transfers between devices: none -> 309 us  [the longest x1 245 us: on_device(): summed = lax.psum_scatter(summed, 'seq', scatter_dimension=0, tiled=True)[0]]
    dot_general x6 -> x0, matrix products: 123 us -> none  [the longest x2 61.4 us: attend(): jnp.einsum('qhk,khd->qhd', weight.astype(jnp.bfloat16), values3, preferre...]
    all_gather x2 -> x1, waiting for transfers between devices: 112 us -> 211 us  [on_device(): q_all = lax.all_gather(queries, 'seq', axis=0, tiled=False)]
    pallas_call x0 -> x2, Pallas kernels: none -> 88.3 us  [the longest x1 57.3 us: on_device(): pl.pallas_call(acc_kernel, grid_spec=pltpu.PrefetchScalarGridSpec(num_sca...]
    pmax x0 -> x1, waiting for transfers between devices: none -> 87.6 us  [on_device(): top = lax.pmax(local_top, 'seq')]
    reduce_sum x6 -> x1, other arithmetic: 48.1 us -> 1.37 us  [on_device(): second = (jnp.sum(my_refresh) >= 2).astype(jnp.int32)]
    all_gather x1 -> x0, local copies, waits for them, and re-layouts: 20.7 us -> none  [on_device(): lax.all_gather(fresh_value, 'seq', axis=0, tiled=True)]
  transfers between devices with their start and end apart: 5 -> 5, of which waited for: 4 -> 5; matrix products, arithmetic and copies ran while one was open for 15% -> 2% of each run, Pallas kernels for 0% -> 0%
where the time goes in v1:
time: 798 us
  waiting for transfers between devices  660 us (83%)
  Pallas kernels  88.3 us (11%)
  matrix products  18.4 us (2%)
  between operations  14.4 us (2%)
  local copies, waits for them, and re-layouts  10.1 us (1%)
    reduce_scatter x1, waiting for transfers between devices, on_device(): summed = lax.psum_scatter(summed, 'seq', scatter_dimension=0, tiled=True)[0]  245 us
    all_gather x1, waiting for transfers between devices, on_device(): q_all = lax.all_gather(queries, 'seq', axis=0, tiled=False)  211 us
    pmax x1, waiting for transfers between devices, on_device(): top = lax.pmax(local_top, 'seq')  87.6 us
    reduce_scatter x1, waiting for transfers between devices, on_device(): total = lax.psum_scatter(total, 'seq', scatter_dimension=0, tiled=True)[0]  64.4 us
    pallas_call x1, Pallas kernels, on_device(): pl.pallas_call(acc_kernel, grid_spec=pltpu.PrefetchScalarGridSpec(num_sca...  57.3 us
    reduce_scatter x1, waiting for transfers between devices, on_device(): lax.psum_scatter(jnp.dot(attended, out_weight, preferred_element_type=jnp...  51.3 us
    pallas_call x1, Pallas kernels, on_device(): pl.pallas_call(max_kernel, grid_spec=pltpu.PrefetchScalarGridSpec(num_sca...  30.9 us
    dot_general x1, matrix products, on_device(): jnp.dot(attended, out_weight, preferred_element_type=jnp.float32)  18.4 us
  transfers between devices with their start and end apart: 5, of which 5 were waited for; matrix products, arithmetic and copies ran while one was open for 2% of the time, Pallas kernels for 0%

profile of v1, /device:TPU:0, one launch (start us, length us, event | category | flops | bytes accessed | tf_op | source)
XLA Modules:
  0.0 797.7 jit_solution(15052390926556125624)
XLA Ops:
  6.5 0.0 all-gather.3.cloned.1.call-start
  6.5 0.7 all-gather.3.cloned.1.call-update
  7.3 0.0 all-reduce.2.cloned.1.call-start
  7.3 1.4 fusion.3
  9.3 0.1 rev.3
  9.4 0.7 iota_reduce_fusion
  10.8 0.8 copy.11
  11.5 0.7 compare_and_fusion
  12.3 0.6 gather_fusion
  12.8 0.7 iota_reduce_fusion.1
  13.6 1.2 pad_add_fusion.fsel_ref
  14.8 0.6 select_reduce_fusion.sval_ref
  15.4 0.6 bitcast_reduce_fusion
  16.0 210.8 %all-gather.3.cloned.1.call-done = bf16[3072,2560]{1,0:T(8,128)(2,1)} async-done(((bf16[384,2560]{1,0:T(8,128)(2,1)}), bf16[3072,2560]{1,0:T(8,128)(2,1)}) %all-gather.3.cloned.1.call-update) | async-done | bytes 15728656 | tf_op jit(solution)/shard_map/all_gather | solution.py:100
  226.7 30.9 %shard_map.91 = f32[8,384,20]{2,1,0:T(8,128)} custom-call(s32[3]{0:T(128)} %pad_add_fusion.fsel_ref, s32[8]{0:T(128)} %get-tuple-element.12.sidx_ref, s32[8]{0:T(128)} %select_reduce_fusion.sval_ref, bf16[8,384,2560]{2,1,0:T(8,128)(2,1)} %bitcast.19, bf16[3,128,2560]{2,1,0:T(8,128)(2,1)} %bitcast.21, bf16[3,128,2560]{2,1,0:T(8,128)(2,1)} %bitcast.22, ...), custom_call_target="tpu_custom_call" | custom-call | tf_op jit(solution)/shard_map/pallas_call | solution.py:114
  257.7 0.0 all-reduce.2.cloned.1.call-update
  257.7 0.0 reduce-scatter.6.cloned.1.call-start
  257.7 87.6 %all-reduce.2.cloned.1.call-done.m_ref = f32[8,384,20]{2,1,0:T(8,128)} async-done(((f32[8,384,20]{2,1,0:T(8,128)}), f32[8,384,20]{2,1,0:T(8,128)}) %all-reduce.2.cloned.1.call-update) | async-done | bytes 245776 | tf_op jit(solution)/shard_map/pmax | solution.py:125
  345.4 57.3 %shard_map.92 = (bf16[8,384,2560]{2,1,0:T(8,128)(2,1)}, f32[8,384,20]{2,1,0:T(8,128)}) custom-call(s32[3]{0:T(128)} %pad_add_fusion.fsel_ref, s32[8]{0:T(128)} %get-tuple-element.12.sidx_ref, s32[8]{0:T(128)} %select_reduce_fusion.sval_ref, bf16[8,384,2560]{2,1,0:T(8,128)(2,1)} %bitcast.20, bf16[3,128,2560]{2,1,0:T(8,128)(2,1)} %bitcast.23, ...), custom_call_target="tpu_custom_call" | custom-call | tf_op jit(solution)/shard_map/pallas_call | solution.py:127
  402.7 0.0 reduce-scatter.6.cloned.1.call-update
  402.7 0.0 reduce-scatter.4.cloned.1.call-start
  402.8 0.5 reduce-scatter.4.cloned.1.call-update
  403.3 0.2 reduce-scatter.8.cloned.1.call-start
  403.5 64.4 %reduce-scatter.6.cloned.1.call-done = f32[1,384,20]{2,1,0:T(8,128)} async-done(((f32[8,384,20]{2,1,0:T(8,128)}), f32[1,384,20]{2,1,0:T(8,128)}) %reduce-scatter.6.cloned.1.call-update) | async-done | bytes 30736 | tf_op jit(solution)/shard_map/reduce_scatter | solution.py:143
  467.9 1.0 copy.12
  468.9 2.2 div.14
  471.1 5.5 copy.13
  476.6 244.9 %reduce-scatter.4.cloned.1.call-done = bf16[1,384,2560]{2,1,0:T(8,128)(2,1)} async-done(((bf16[8,384,2560]{2,1,0:T(8,128)(2,1)}), bf16[1,384,2560]{2,1,0:T(8,128)(2,1)}) %reduce-scatter.4.cloned.1.call-update) | async-done | bytes 1966096 | tf_op jit(solution)/shard_map/reduce_scatter | solution.py:142
  721.5 18.4 %convolution_convert_fusion = bf16[384,5120]{1,0:T(8,128)(2,1)} fusion(bf16[2560,5120]{1,0:T(8,128)(2,1)} %param.17, f32[384,2560]{1,0:T(8,128)} %copy.13, bf16[1,384,2560]{2,1,0:T(8,128)(2,1)} %reduce-scatter.4.cloned.1.call-done), kind=kOutput, calls=%fused_computation.1 | convolution fusion | flops 10071244800 | bytes 36044800 | tf_op jit(solution)/shard_map/dot_general | solution.py:150
  739.8 0.0 reduce-scatter.8.cloned.1.call-update
  739.9 51.3 %reduce-scatter.8.cloned.1.call-done = bf16[192,5120]{1,0:T(8,128)(2,1)} async-done(((bf16[384,5120]{1,0:T(8,128)(2,1)}), bf16[192,5120]{1,0:T(8,128)(2,1)}) %reduce-scatter.8.cloned.1.call-update) | async-done | bytes 1966096 | tf_op jit(solution)/shard_map/reduce_scatter | solution.py:149
  (1 shorter events, 0.0 us)
Async XLA Ops:
  6.5 220.2 %all-gather.3.cloned.1.call-start = ((), (), s32[]{:S(2)}) async-start(), calls=%async_computation.7 | async-start | bytes 17694720 | tf_op jit(solution)/shard_map/all_gather | solution.py:100
  7.3 338.1 %all-reduce.2.cloned.1.call-start = ((), (), s32[]{:S(2)}) async-start(), calls=%async_computation.3 | async-start | bytes 3145728 | tf_op jit(solution)/shard_map/pmax | solution.py:125
  257.7 210.2 %reduce-scatter.6.cloned.1.call-start = ((), (), s32[]{:S(2)}) async-start(), calls=%async_computation.5 | async-start | bytes 1769472 | tf_op jit(solution)/shard_map/reduce_scatter | solution.py:143
  402.7 318.7 %reduce-scatter.4.cloned.1.call-start = ((), (), s32[]{:S(2)}) async-start(), calls=%async_computation.4 | async-start | bytes 17694720 | tf_op jit(solution)/shard_map/reduce_scatter | solution.py:142
  403.3 387.9 %reduce-scatter.8.cloned.1.call-start = ((), (), s32[]{:S(2)}) async-start(), calls=%async_computation.6 | async-start | bytes 5898240 | tf_op jit(solution)/shard_map/reduce_scatter | solution.py:149
Sparse Core Ops, SparseCore 0:
  9.5 217.1 all-gather.2
  257.8 87.5 all-reduce.1
  402.9 65.0 reduce-scatter.5
  471.4 250.0 reduce-scatter.3
  740.0 51.1 reduce-scatter.7

commit v2 on v1

--- a/solution.py
+++ b/solution.py
@@ -17,9 +17,9 @@
     qj = q_ref[0, :, sl]
     dims = (((1,), (1,)), ((), ()))
     scale = HD ** -0.5
-    s0 = lax.dot_general(qj, kf0_ref[0, :, sl], dims, preferred_element_type=jnp.float32) * scale
-    s1 = lax.dot_general(qj, kf1_ref[0, :, sl], dims, preferred_element_type=jnp.float32) * scale
-    s2 = lax.dot_general(qj, ks_ref[0, :, sl], dims, preferred_element_type=jnp.float32) * scale
+    s0 = lax.dot_general(kf0_ref[0, :, sl], qj, dims, preferred_element_type=jnp.float32) * scale
+    s1 = lax.dot_general(kf1_ref[0, :, sl], qj, dims, preferred_element_type=jnp.float32) * scale
+    s2 = lax.dot_general(ks_ref[0, :, sl], qj, dims, preferred_element_type=jnp.float32) * scale
     s1 = jnp.where(second > 0, s1, NEG)
     s2 = jnp.where(valid > 0, s2, NEG)
     return s0, s1, s2
@@ -33,10 +33,10 @@
     for j in range(heads_here):
         s0, s1, s2 = _scores(q_ref, kf0_ref, kf1_ref, ks_ref, j, second, valid)
         m = jnp.maximum(
-            jnp.maximum(jnp.max(s0, axis=1, keepdims=True), jnp.max(s1, axis=1, keepdims=True)),
-            jnp.max(s2, axis=1, keepdims=True),
+            jnp.maximum(jnp.max(s0, axis=0, keepdims=True), jnp.max(s1, axis=0, keepdims=True)),
+            jnp.max(s2, axis=0, keepdims=True),
         )
-        m_ref[0, :, j : j + 1] = m
+        m_ref[0, j : j + 1, :] = m
 
 
 def acc_kernel(
@@ -47,25 +47,26 @@
     heads_here = q_ref.shape[2] // HD
     second = fsel_ref[2]
     valid = sval_ref[r]
+    tn = (((0,), (0,)), ((), ()))
     for j in range(heads_here):
         sl = slice(j * HD, (j + 1) * HD)
         s0, s1, s2 = _scores(q_ref, kf0_ref, kf1_ref, ks_ref, j, second, valid)
-        top = m_ref[0, :, j : j + 1]
+        top = m_ref[0, j : j + 1, :]
         w0 = jnp.exp(s0 - top)
         w1 = jnp.exp(s1 - top)
         w2 = jnp.exp(s2 - top)
         total = (
-            jnp.sum(w0, axis=1, keepdims=True)
-            + jnp.sum(w1, axis=1, keepdims=True)
-            + jnp.sum(w2, axis=1, keepdims=True)
+            jnp.sum(w0, axis=0, keepdims=True)
+            + jnp.sum(w1, axis=0, keepdims=True)
+            + jnp.sum(w2, axis=0, keepdims=True)
         )
         summed = (
-            jnp.dot(w0.astype(jnp.bfloat16), vf0_ref[0, :, sl], preferred_element_type=jnp.float32)
-            + jnp.dot(w1.astype(jnp.bfloat16), vf1_ref[0, :, sl], preferred_element_type=jnp.float32)
-            + jnp.dot(w2.astype(jnp.bfloat16), vs_ref[0, :, sl], preferred_element_type=jnp.float32)
+            lax.dot_general(w0.astype(jnp.bfloat16), vf0_ref[0, :, sl], tn, preferred_element_type=jnp.float32)
+            + lax.dot_general(w1.astype(jnp.bfloat16), vf1_ref[0, :, sl], tn, preferred_element_type=jnp.float32)
+            + lax.dot_general(w2.astype(jnp.bfloat16), vs_ref[0, :, sl], tn, preferred_element_type=jnp.float32)
         )
         acc_ref[0, :, sl] = summed.astype(acc_ref.dtype)
-        l_ref[0, :, j : j + 1] = total
+        l_ref[0, j : j + 1, :] = total
 
 
 def on_device(
@@ -107,8 +108,8 @@
     f0_spec = pl.BlockSpec((1, TILE, width_here), lambda r, f, s, v: (f[0], 0, 0))
     f1_spec = pl.BlockSpec((1, TILE, width_here), lambda r, f, s, v: (f[1], 0, 0))
     s_spec = pl.BlockSpec((1, TILE, width_here), lambda r, f, s, v: (s[r], 0, 0))
-    stat_spec = pl.BlockSpec((1, tokens_here, heads_here), lambda r, f, s, v: (r, 0, 0))
-    stat_shape = jax.ShapeDtypeStruct((readers, tokens_here, heads_here), jnp.float32)
+    stat_spec = pl.BlockSpec((1, heads_here, tokens_here), lambda r, f, s, v: (r, 0, 0))
+    stat_shape = jax.ShapeDtypeStruct((readers, heads_here, tokens_here), jnp.float32)
     params = pltpu.CompilerParams(dimension_semantics=("arbitrary",))
 
     local_top = pl.pallas_call(
@@ -140,7 +141,7 @@
     )(fsel, sidx, sval, q_all, fk3, fk3, sk3, fv3, fv3, sv3, top)
 
     summed = lax.psum_scatter(summed, "seq", scatter_dimension=0, tiled=True)[0]
-    total = lax.psum_scatter(total, "seq", scatter_dimension=0, tiled=True)[0]
+    total = lax.psum_scatter(total, "seq", scatter_dimension=0, tiled=True)[0].T
     attended = (
         (summed.astype(jnp.float32).reshape(tokens_here, heads_here, HD) / total[:, :, None])
         .reshape(tokens_here, width_here)

time: 798 us -> 753 us (0.944)
  waiting for transfers between devices: 660 us -> 637 us
  Pallas kernels: 88.3 us -> 67.4 us
    reduce_scatter x1 -> x0, waiting for transfers between devices: 64.4 us -> none  [on_device(): total = lax.psum_scatter(total, 'seq', scatter_dimension=0, tiled=True)[0]]
    unnamed x5 -> x6, waiting for transfers between devices: 1.28 us -> 59.6 us
    pmax x1, waiting for transfers between devices: 87.6 us -> 70 us  [on_device(): top = lax.pmax(local_top, 'seq')]
    pallas_call x1, Pallas kernels: 57.3 us -> 43.2 us  [on_device(): pl.pallas_call(acc_kernel, grid_spec=pltpu.PrefetchScalarGridSpec(num_sca...]
where the time goes in v2:
time: 753 us
  waiting for transfers between devices  637 us (85%)
  Pallas kernels  67.4 us (9%)
  matrix products  18.4 us (2%)
  between operations  14.4 us (2%)
  local copies, waits for them, and re-layouts  9.81 us (1%)
    reduce_scatter x1, waiting for transfers between devices, on_device(): summed = lax.psum_scatter(summed, 'seq', scatter_dimension=0, tiled=True)[0]  245 us
    all_gather x1, waiting for transfers between devices, on_device(): q_all = lax.all_gather(queries, 'seq', axis=0, tiled=False)  211 us
    pmax x1, waiting for transfers between devices, on_device(): top = lax.pmax(local_top, 'seq')  70 us
    unnamed x6, waiting for transfers between devices  59.6 us
    reduce_scatter x1, waiting for transfers between devices, on_device(): lax.psum_scatter(jnp.dot(attended, out_weight, preferred_element_type=jnp...  51.4 us
    pallas_call x1, Pallas kernels, on_device(): pl.pallas_call(acc_kernel, grid_spec=pltpu.PrefetchScalarGridSpec(num_sca...  43.2 us
    pallas_call x1, Pallas kernels, on_device(): pl.pallas_call(max_kernel, grid_spec=pltpu.PrefetchScalarGridSpec(num_sca...  24.2 us
    dot_general x1, matrix products, on_device(): jnp.dot(attended, out_weight, preferred_element_type=jnp.float32)  18.4 us
  transfers between devices with their start and end apart: 5, of which 5 were waited for; matrix products, arithmetic and copies ran while one was open for 2% of the time, Pallas kernels for 0%

profile of v2, /device:TPU:0, one launch (start us, length us, event | category | flops | bytes accessed | tf_op | source)
XLA Modules:
  0.0 753.3 jit_solution(16951174944705257681)
XLA Ops:
  6.5 0.0 all-gather.3.cloned.1.call-start
  6.5 0.7 all-gather.3.cloned.1.call-update
  7.3 0.0 all-reduce.3.cloned.1.call-start
  7.3 1.4 fusion.3
  9.3 0.1 rev.3
  9.4 0.7 iota_reduce_fusion
  10.8 0.8 copy.14
  11.5 0.7 compare_and_fusion
  12.3 0.6 gather_fusion
  12.8 0.7 iota_reduce_fusion.1
  13.6 1.3 pad_add_fusion.fsel_ref
  14.9 0.7 select_reduce_fusion.sval_ref
  15.5 0.7 bitcast_reduce_fusion
  16.2 210.5 %all-gather.3.cloned.1.call-done = bf16[3072,2560]{1,0:T(8,128)(2,1)} async-done(((bf16[384,2560]{1,0:T(8,128)(2,1)}), bf16[3072,2560]{1,0:T(8,128)(2,1)}) %all-gather.3.cloned.1.call-update) | async-done | bytes 15728656 | tf_op jit(solution)/shard_map/all_gather | solution.py:101
  226.7 24.2 %shard_map.91 = f32[8,20,384]{2,1,0:T(8,128)} custom-call(s32[3]{0:T(128)} %pad_add_fusion.fsel_ref, s32[8]{0:T(128)} %get-tuple-element.12.sidx_ref, s32[8]{0:T(128)} %select_reduce_fusion.sval_ref, bf16[8,384,2560]{2,1,0:T(8,128)(2,1)} %bitcast.22, bf16[3,128,2560]{2,1,0:T(8,128)(2,1)} %bitcast.24, bf16[3,128,2560]{2,1,0:T(8,128)(2,1)} %bitcast.25, ...), custom_call_target="tpu_custom_call" | custom-call | tf_op jit(solution)/shard_map/pallas_call | solution.py:115
  250.9 0.0 all-reduce.3.cloned.1.call-update
  250.9 0.0 reduce-scatter.10.cloned.1.call-start
  251.0 70.0 %all-reduce.3.cloned.1.call-done.m_ref = f32[8,20,384]{2,1,0:T(8,128)} async-done(((f32[8,20,384]{2,1,0:T(8,128)}), f32[8,20,384]{2,1,0:T(8,128)}) %all-reduce.3.cloned.1.call-update) | async-done | bytes 245776 | tf_op jit(solution)/shard_map/pmax | solution.py:126
  321.0 43.2 %shard_map.92 = (bf16[8,384,2560]{2,1,0:T(8,128)(2,1)}, f32[8,20,384]{2,1,0:T(8,128)}) custom-call(s32[3]{0:T(128)} %pad_add_fusion.fsel_ref, s32[8]{0:T(128)} %get-tuple-element.12.sidx_ref, s32[8]{0:T(128)} %select_reduce_fusion.sval_ref, bf16[8,384,2560]{2,1,0:T(8,128)(2,1)} %bitcast.23, bf16[3,128,2560]{2,1,0:T(8,128)(2,1)} %bitcast.26, ...), custom_call_target="tpu_custom_call" | custom-call | tf_op jit(solution)/shard_map/pallas_call | solution.py:128
  364.3 0.0 reduce-scatter.10.cloned.1.call-update
  364.3 0.0 reduce-scatter.6.cloned.1.call-start
  364.3 0.5 reduce-scatter.6.cloned.1.call-update
  364.9 0.0 reduce-scatter.8.cloned.1.call-start
  364.9 58.4 %reduce-scatter.10.cloned.1.call-done = f32[1,20,384]{2,1,0:T(8,128)} async-done(((f32[8,20,384]{2,1,0:T(8,128)}), f32[1,20,384]{2,1,0:T(8,128)}) %reduce-scatter.10.cloned.1.call-update) | async-done | bytes 30736
  423.3 2.9 div.11
  426.2 5.5 copy.15
  431.7 245.4 %reduce-scatter.6.cloned.1.call-done = bf16[1,384,2560]{2,1,0:T(8,128)(2,1)} async-done(((bf16[8,384,2560]{2,1,0:T(8,128)(2,1)}), bf16[1,384,2560]{2,1,0:T(8,128)(2,1)}) %reduce-scatter.6.cloned.1.call-update) | async-done | bytes 1966096 | tf_op jit(solution)/shard_map/reduce_scatter | solution.py:143
  677.1 18.4 %convolution_convert_fusion = bf16[384,5120]{1,0:T(8,128)(2,1)} fusion(bf16[2560,5120]{1,0:T(8,128)(2,1)} %param.17, f32[384,2560]{1,0:T(8,128)} %copy.15, bf16[1,384,2560]{2,1,0:T(8,128)(2,1)} %reduce-scatter.6.cloned.1.call-done), kind=kOutput, calls=%fused_computation.1 | convolution fusion | flops 10071244800 | bytes 36044800 | tf_op jit(solution)/shard_map/dot_general | solution.py:151
  695.4 0.0 reduce-scatter.8.cloned.1.call-update
  695.5 51.4 %reduce-scatter.8.cloned.1.call-done = bf16[192,5120]{1,0:T(8,128)(2,1)} async-done(((bf16[384,5120]{1,0:T(8,128)(2,1)}), bf16[192,5120]{1,0:T(8,128)(2,1)}) %reduce-scatter.8.cloned.1.call-update) | async-done | bytes 1966096 | tf_op jit(solution)/shard_map/reduce_scatter | solution.py:150
  (1 shorter events, 0.0 us)
Async XLA Ops:
  6.5 220.2 %all-gather.3.cloned.1.call-start = ((), (), s32[]{:S(2)}) async-start(), calls=%async_computation.6 | async-start | bytes 17694720 | tf_op jit(solution)/shard_map/all_gather | solution.py:101
  7.3 313.8 %all-reduce.3.cloned.1.call-start = ((), (), s32[]{:S(2)}) async-start(), calls=%async_computation.3 | async-start | bytes 589824 | tf_op jit(solution)/shard_map/pmax | solution.py:126
  250.9 172.3 %reduce-scatter.10.cloned.1.call-start = ((), (), s32[]{:S(2)}) async-start(), calls=%async_computation.7 | async-start | bytes 331776
  364.3 312.8 %reduce-scatter.6.cloned.1.call-start = ((), (), s32[]{:S(2)}) async-start(), calls=%async_computation.4 | async-start | bytes 17694720 | tf_op jit(solution)/shard_map/reduce_scatter | solution.py:143
  364.9 381.9 %reduce-scatter.8.cloned.1.call-start = ((), (), s32[]{:S(2)}) async-start(), calls=%async_computation.5 | async-start | bytes 5898240 | tf_op jit(solution)/shard_map/reduce_scatter | solution.py:150
Sparse Core Ops, SparseCore 0:
  9.5 217.1 all-gather.2
  251.1 69.9 all-reduce.2
  364.4 58.8 reduce-scatter.9
  426.7 250.3 reduce-scatter.5
  695.6 51.1 reduce-scatter.7

commit v3 on v2

--- a/solution.py
+++ b/solution.py
@@ -25,23 +25,9 @@
     return s0, s1, s2
 
 
-def max_kernel(fsel_ref, sidx_ref, sval_ref, q_ref, kf0_ref, kf1_ref, ks_ref, m_ref):
-    r = pl.program_id(0)
-    heads_here = q_ref.shape[2] // HD
-    second = fsel_ref[2]
-    valid = sval_ref[r]
-    for j in range(heads_here):
-        s0, s1, s2 = _scores(q_ref, kf0_ref, kf1_ref, ks_ref, j, second, valid)
-        m = jnp.maximum(
-            jnp.maximum(jnp.max(s0, axis=0, keepdims=True), jnp.max(s1, axis=0, keepdims=True)),
-            jnp.max(s2, axis=0, keepdims=True),
-        )
-        m_ref[0, j : j + 1, :] = m
-
-
 def acc_kernel(
-    fsel_ref, sidx_ref, sval_ref, q_ref, kf0_ref, kf1_ref, ks_ref, vf0_ref, vf1_ref, vs_ref, m_ref,
-    acc_ref, l_ref,
+    fsel_ref, sidx_ref, sval_ref, q_ref, kf0_ref, kf1_ref, ks_ref, vf0_ref, vf1_ref, vs_ref,
+    acc_ref, m_ref, l_ref,
 ):
     r = pl.program_id(0)
     heads_here = q_ref.shape[2] // HD
@@ -51,7 +37,10 @@
     for j in range(heads_here):
         sl = slice(j * HD, (j + 1) * HD)
         s0, s1, s2 = _scores(q_ref, kf0_ref, kf1_ref, ks_ref, j, second, valid)
-        top = m_ref[0, j : j + 1, :]
+        top = jnp.maximum(
+            jnp.maximum(jnp.max(s0, axis=0, keepdims=True), jnp.max(s1, axis=0, keepdims=True)),
+            jnp.max(s2, axis=0, keepdims=True),
+        )
         w0 = jnp.exp(s0 - top)
         w1 = jnp.exp(s1 - top)
         w2 = jnp.exp(s2 - top)
@@ -66,7 +55,29 @@
             + lax.dot_general(w2.astype(jnp.bfloat16), vs_ref[0, :, sl], tn, preferred_element_type=jnp.float32)
         )
         acc_ref[0, :, sl] = summed.astype(acc_ref.dtype)
+        m_ref[0, j : j + 1, :] = top
         l_ref[0, j : j + 1, :] = total
+
+
+def ring_order(n):
+    if n == 8:
+        return [0, 2, 4, 6, 7, 5, 3, 1]
+    return list(range(n))
+
+
+def combine(run, mine):
+    acc_r, stat_r = run
+    acc_o, stat_o = mine
+    tokens, width = acc_o.shape
+    hh = width // HD
+    top = jnp.maximum(stat_r[0], stat_o[0])
+    f_r = jnp.exp(stat_r[0] - top)
+    f_o = jnp.exp(stat_o[0] - top)
+    total = stat_r[1] * f_r + stat_o[1] * f_o
+    acc = acc_r.astype(jnp.float32).reshape(tokens, hh, HD) * f_r.T[:, :, None] + acc_o.astype(
+        jnp.float32
+    ).reshape(tokens, hh, HD) * f_o.T[:, :, None]
+    return acc.reshape(tokens, width), jnp.stack([top, total])
 
 
 def on_device(
@@ -112,38 +123,53 @@
     stat_shape = jax.ShapeDtypeStruct((readers, heads_here, tokens_here), jnp.float32)
     params = pltpu.CompilerParams(dimension_semantics=("arbitrary",))
 
-    local_top = pl.pallas_call(
-        max_kernel,
-        grid_spec=pltpu.PrefetchScalarGridSpec(
-            num_scalar_prefetch=3,
-            grid=(readers,),
-            in_specs=[q_spec, f0_spec, f1_spec, s_spec],
-            out_specs=stat_spec,
-        ),
-        out_shape=stat_shape,
-        compiler_params=params,
-    )(fsel, sidx, sval, q_all, fk3, fk3, sk3)
-    top = lax.pmax(local_top, "seq")
-
-    summed, total = pl.pallas_call(
+    summed, top, total = pl.pallas_call(
         acc_kernel,
         grid_spec=pltpu.PrefetchScalarGridSpec(
             num_scalar_prefetch=3,
             grid=(readers,),
-            in_specs=[q_spec, f0_spec, f1_spec, s_spec, f0_spec, f1_spec, s_spec, stat_spec],
-            out_specs=[q_spec, stat_spec],
+            in_specs=[q_spec, f0_spec, f1_spec, s_spec, f0_spec, f1_spec, s_spec],
+            out_specs=[q_spec, stat_spec, stat_spec],
         ),
         out_shape=[
             jax.ShapeDtypeStruct((readers, tokens_here, width_here), jnp.bfloat16),
             stat_shape,
+            stat_shape,
         ],
         compiler_params=params,
-    )(fsel, sidx, sval, q_all, fk3, fk3, sk3, fv3, fv3, sv3, top)
-
-    summed = lax.psum_scatter(summed, "seq", scatter_dimension=0, tiled=True)[0]
-    total = lax.psum_scatter(total, "seq", scatter_dimension=0, tiled=True)[0].T
+    )(fsel, sidx, sval, q_all, fk3, fk3, sk3, fv3, fv3, sv3)
+    stats = jnp.stack([top, total], axis=1)
+
+    ring = ring_order(readers)
+    place = [0] * readers
+    for i, d in enumerate(ring):
+        place[d] = i
+    ring_arr = jnp.array(ring, jnp.int32)
+    pos = jnp.array(place, jnp.int32)[me]
+    forward = [(ring[i], ring[(i + 1) % readers]) for i in range(readers)]
+    backward = [(ring[i], ring[(i - 1) % readers]) for i in range(readers)]
+    split = heads_here // 2
+
+    def own(at, h0, h1):
+        r = ring_arr[at % readers]
+        acc = lax.dynamic_index_in_dim(summed, r, 0, keepdims=False)[:, h0 * HD : h1 * HD]
+        st = lax.dynamic_index_in_dim(stats, r, 0, keepdims=False)[:, h0:h1]
+        return acc, st
+
+    run_f = own(pos - 1 + readers, 0, split)
+    run_b = own(pos + 1, split, heads_here)
+    for k in range(1, readers):
+        got_f = lax.ppermute(run_f, "seq", forward)
+        got_b = lax.ppermute(run_b, "seq", backward)
+        run_f = combine(got_f, own(pos - 1 - k + 2 * readers, 0, split))
+        run_b = combine(got_b, own(pos + 1 + k, split, heads_here))
+        if k < readers - 1:
+            run_f = (run_f[0].astype(jnp.bfloat16), run_f[1])
+            run_b = (run_b[0].astype(jnp.bfloat16), run_b[1])
+    acc = jnp.concatenate([run_f[0], run_b[0]], axis=1)
+    total = jnp.concatenate([run_f[1][1], run_b[1][1]], axis=0).T
     attended = (
-        (summed.astype(jnp.float32).reshape(tokens_here, heads_here, HD) / total[:, :, None])
+        (acc.reshape(tokens_here, heads_here, HD) / total[:, :, None])
         .reshape(tokens_here, width_here)
         .astype(jnp.bfloat16)
     )

time: 753 us -> 681 us (0.904); the launches traced: 753 us -> 673 us
  waiting for transfers between devices: 637 us -> 311 us
  local copies, waits for them, and re-layouts: 9.81 us -> 151 us
  other arithmetic: 6.18 us -> 45.7 us
  between operations: 14.4 us -> 51 us
  starting transfers between devices: 0.16 us -> 30.7 us
    reduce_scatter x1 -> x0, waiting for transfers between devices: 245 us -> none  [on_device(): summed = lax.psum_scatter(summed, 'seq', scatter_dimension=0, tiled=True)[0]]
    mul x0 -> x56, local copies, waits for them, and re-layouts: none -> 120 us  [the longest x28 60.1 us: combine(): acc_o.astype(jnp.float32).reshape(tokens, hh, HD) * f_o.T[:, :, None]]
    ppermute x0 -> x28, waiting for transfers between devices: none -> 82.7 us  [the longest x14 74.4 us: on_device(): got_b = lax.ppermute(run_b, 'seq', backward)]
    pmax x1 -> x0, waiting for transfers between devices: 70 us -> none  [on_device(): top = lax.pmax(local_top, 'seq')]
    unnamed x6 -> x2, waiting for transfers between devices: 59.6 us -> 0.7 us
    all_gather x1, waiting for transfers between devices: 211 us -> 176 us  [on_device(): q_all = lax.all_gather(queries, 'seq', axis=0, tiled=False)]
    ppermute x0 -> x28, starting transfers between devices: none -> 30.6 us  [the longest x14 16.2 us: on_device(): got_f = lax.ppermute(run_f, 'seq', forward)]
    pallas_call x1 -> x0, Pallas kernels: 24.2 us -> none  [on_device(): pl.pallas_call(max_kernel, grid_spec=pltpu.PrefetchScalarGridSpec(num_sca...]
  transfers between devices with their start and end apart: 5 -> 30, of which waited for: 5 -> 13; matrix products, arithmetic and copies ran while one was open for 2% -> 26% of each run, Pallas kernels for 0% -> 0%
where the time goes in v3:
time: 681 us; the launch traced here: 673 us
  waiting for transfers between devices  311 us (46%)
  local copies, waits for them, and re-layouts  151 us (22%)
  Pallas kernels  66.3 us (10%)
  between operations  51 us (7%)
  other arithmetic  45.7 us (7%)
  starting transfers between devices  30.7 us (5%)
  matrix products  16.9 us (2%)
    all_gather x1, waiting for transfers between devices, on_device(): q_all = lax.all_gather(queries, 'seq', axis=0, tiled=False)  176 us
    ppermute x14, waiting for transfers between devices, on_device(): got_b = lax.ppermute(run_b, 'seq', backward)  74.4 us
    pallas_call x1, Pallas kernels, on_device(): pl.pallas_call(acc_kernel, grid_spec=pltpu.PrefetchScalarGridSpec(num_sca...  66.3 us
    mul x28, local copies, waits for them, and re-layouts, combine(): acc_o.astype(jnp.float32).reshape(tokens, hh, HD) * f_o.T[:, :, None]  60.1 us
    mul x28, local copies, waits for them, and re-layouts, combine(): acc_r.astype(jnp.float32).reshape(tokens, hh, HD) * f_r.T[:, :, None]  60 us
    reduce_scatter x1, waiting for transfers between devices, on_device(): lax.psum_scatter(jnp.dot(attended, out_weight, preferred_element_type=jnp...  51.2 us
    squeeze x1, local copies, waits for them, and re-layouts, own(): lax.dynamic_index_in_dim(summed, r, 0, keepdims=False)[:, h0 * HD:h1 * HD]  17.3 us
    dot_general x1, matrix products, on_device(): jnp.dot(attended, out_weight, preferred_element_type=jnp.float32)  16.9 us
  transfers between devices with their start and end apart: 30, of which 13 were waited for; matrix products, arithmetic and copies ran while one was open for 26% of the time, Pallas kernels for 0%

profile of v3, /device:TPU:0, one launch (start us, length us, event | category | flops | bytes accessed | tf_op | source)
XLA Modules:
  0.0 672.6 jit_solution(15951896018658121362)
XLA Ops:
  50.7 176.1 %all-gather.3.cloned.1.call-done = bf16[3072,2560]{1,0:T(8,128)(2,1)} async-done(((bf16[384,2560]{1,0:T(8,128)(2,1)}), bf16[3072,2560]{1,0:T(8,128)(2,1)}) %all-gather.3.cloned.1.call-update) | async-done | bytes 15728656 | tf_op jit(solution)/shard_map/all_gather | solution.py:112
  226.8 66.3 %shard_map.109 = (bf16[8,384,2560]{2,1,0:T(8,128)(2,1)}, f32[8,20,384]{2,1,0:T(8,128)}, f32[8,20,384]{2,1,0:T(8,128)}) custom-call(s32[3]{0:T(128)} %pad_add_fusion.fsel_ref, s32[8]{0:T(128)} %get-tuple-element.13.sidx_ref, s32[8]{0:T(128)} %select_reduce_fusion.sval_ref, bf16[8,384,2560]{2,1,0:T(8,128)(2,1)} %bitcast.339, bf16[3,128,2560]{2,1,0:T(8,128)(2,1)} %bitcast.340, ...), custom_call_target="tpu_custom_call" | custom-call | tf_op jit(solution)/shard_map/pallas_call | solution.py:126
  298.6 17.3 %dynamic-slice_bitcast_fusion.7 = (bf16[384,2560]{1,0:T(8,128)(2,1)}, bf16[384,2560]{1,0:T(8,128)(2,1)}, bf16[384,2560]{1,0:T(8,128)(2,1)}, bf16[384,2560]{1,0:T...) fusion(bf16[8,384,2560]{2,1,0:T(8,128)(2,1)} %get-tuple-element, ...), kind=kLoop, calls=%fused_computation.48 | loop fusion | bytes 55050296 | tf_op jit(solution)/shard_map/jit(dynamic_index_in_dim)/squeeze | solution.py:155
  325.1 16.6 %collective-permute-done.17 = f32[2,10,384]{2,1,0:T(8,128)S(1)} collective-permute-done((f32[2,10,384]{2,1,0:T(8,128)S(1)}, f32[2,10,384]{2,1,0:T(8,128)S(1)}, u32[]{:S(2)}, u32[]{:S(2)}) %collective-permute-start.17) | collective-permute-done | bytes 30752 | tf_op jit(solution)/shard_map/ppermute | solution.py:163
  347.3 2.9 copy.63
  351.7 3.0 copy.64
  360.3 2.9 copy.66
  364.6 2.9 copy.48
  368.9 3.0 copy.49
  377.5 2.9 copy.51
  387.4 2.9 copy.67
  401.6 2.9 copy.52
  405.9 2.9 copy.53
  417.3 3.2 add_convert_fusion.5
  425.3 16.6 %collective-permute-done.16 = bf16[384,1280]{1,0:T(8,128)(2,1)S(1)} collective-permute-done((bf16[384,1280]{1,0:T(8,128)(2,1)S(1)}, bf16[384,1280]{1,0:T(8,128)(2,1)S(1)}, u32[]{:S(2)}, u32[]{:S(2)}) %collective-permute-start.16) | collective-permute-done | bytes 983072 | tf_op jit(solution)/shard_map/ppermute | solution.py:163
  446.6 17.2 %collective-permute-done.18 = bf16[384,1280]{1,0:T(8,128)(2,1)S(1)} collective-permute-done((bf16[384,1280]{1,0:T(8,128)(2,1)S(1)}, bf16[384,1280]{1,0:T(8,128)(2,1)S(1)}, u32[]{:S(2)}, u32[]{:S(2)}) %collective-permute-start.18) | collective-permute-done | bytes 983072 | tf_op jit(solution)/shard_map/ppermute | solution.py:163
  475.0 2.9 copy.70
  495.8 3.2 add_convert_fusion.2
  504.7 15.8 %collective-permute-done.22 = bf16[384,1280]{1,0:T(8,128)(2,1)S(1)} collective-permute-done((bf16[384,1280]{1,0:T(8,128)(2,1)S(1)}, bf16[384,1280]{1,0:T(8,128)(2,1)S(1)}, u32[]{:S(2)}, u32[]{:S(2)}) %collective-permute-start.22) | collective-permute-done | bytes 983072 | tf_op jit(solution)/shard_map/ppermute | solution.py:163
  526.6 2.9 copy.73
  530.9 2.9 copy.74
  535.3 2.9 copy.58
  542.5 3.2 add_convert_fusion
  553.5 8.2 %collective-permute-done.27 = f32[2,10,384]{2,1,0:T(8,128)S(1)} collective-permute-done((f32[2,10,384]{2,1,0:T(8,128)S(1)}, f32[2,10,384]{2,1,0:T(8,128)S(1)}, u32[]{:S(2)}, u32[]{:S(2)}) %collective-permute-start.27) | collective-permute-done | bytes 30752 | tf_op jit(solution)/shard_map/ppermute | solution.py:163
  561.7 4.3 collective-permute-done.13
  567.4 2.9 copy.60
  571.7 2.9 copy.61
  580.3 2.9 copy.76
  583.2 6.6 multiply_add_fusion.1
  589.7 3.0 copy.77
  597.1 16.9 %convolution_convert_fusion = bf16[384,5120]{1,0:T(8,128)(2,1)} fusion(bf16[384,2560]{0,1:T(8,128)(2,1)S(1)} %bitcast.382, bf16[2560,5120]{1,0:T(8,128)(2,1)} %param.19), kind=kOutput, calls=%fused_computation.1 | convolution fusion | flops 10068295680 | bytes 32112640 | tf_op jit(solution)/shard_map/dot_general | solution.py:177
  614.1 51.2 %reduce-scatter.2.cloned.1.call-done = bf16[192,5120]{1,0:T(8,128)(2,1)} async-done(((bf16[384,5120]{1,0:T(8,128)(2,1)}), bf16[192,5120]{1,0:T(8,128)(2,1)}) %reduce-scatter.2.cloned.1.call-update) | async-done | bytes 1966096 | tf_op jit(solution)/shard_map/reduce_scatter | solution.py:176
  (263 shorter events, 149.3 us)
Async XLA Ops:
  6.5 31.6 %copy-start.48 = (s32[8,24]{1,0:T(8,128)S(1)}, s32[8,24]{1,0:T(8,128)}, u32[]{:S(2)}) copy-start(s32[8,24]{1,0:T(8,128)} %param.18) | copy-start | bytes 2308
  6.5 35.4 %copy-start.50 = (s32[24]{0:T(128)S(1)}, s32[24]{0:T(128)}, u32[]{:S(2)}) copy-start(s32[24]{0:T(128)} %param.16) | copy-start | bytes 292
  6.5 220.3 %all-gather.3.cloned.1.call-start = ((), (), s32[]{:S(2)}) async-start(), calls=%async_computation.2 | async-start | bytes 17694720 | tf_op jit(solution)/shard_map/all_gather | solution.py:112
  7.3 658.0 %reduce-scatter.2.cloned.1.call-start = ((), (), s32[]{:S(2)}) async-start(), calls=%async_computation.1 | async-start | bytes 5898240 | tf_op jit(solution)/shard_map/reduce_scatter | solution.py:176
  295.4 26.5 %collective-permute-start.15 = (f32[2,10,384]{2,1,0:T(8,128)}, f32[2,10,384]{2,1,0:T(8,128)}, u32[]{:S(2)}, u32[]{:S(2)}) collective-permute-start(f32[2,10,384]{2,1,0:T(8,128)} %slice.404), channel_id=1, source_target_pairs={{0,4},{8,0},{16,8},{24,16},{28,24},{20,28},{12,20},{4,12},{1,5},{9... | collective-permute-start | bytes 92168 | tf_op jit(solution)/shard_map/ppermute | solution.py:163
  318.3 99.0 %collective-permute-start.14 = (bf16[384,1280]{1,0:T(8,128)(2,1)}, bf16[384,1280]{1,0:T(8,128)(2,1)}, u32[]{:S(2)}, u32[]{:S(2)}) collective-permute-start(bf16[384,1280]{1,0:T(8,128)(2,1)} %slice.403), channel_id=1, source_target_pairs={{0,4},{8,0},{16,8},{24,16},{28,24},{20,28},{12,20},{4,12},{1,5},{9... | collective-permute-start | bytes 2949128 | tf_op jit(solution)/shard_map/ppermute | solution.py:163
  318.4 5.9 collective-permute-start.1
  321.4 100.1 %collective-permute-start = (bf16[384,1280]{1,0:T(8,128)(2,1)}, bf16[384,1280]{1,0:T(8,128)(2,1)S(1)}, u32[]{:S(2)}, u32[]{:S(2)}) collective-permute-start(bf16[384,1280]{1,0:T(8,128)(2,1)} %slice.368), channel_id=1, source_target_pairs={{0,8},{8,16},{16,24},{24,28},{28,20},{20,12},{12,4},{4,0},{1,9},{9... | collective-permute-start | bytes 2949128 | tf_op jit(solution)/shard_map/ppermute | solution.py:162
  322.7 19.0 %collective-permute-start.17 = (f32[2,10,384]{2,1,0:T(8,128)S(1)}, f32[2,10,384]{2,1,0:T(8,128)S(1)}, u32[]{:S(2)}, u32[]{:S(2)}) collective-permute-start(f32[2,10,384]{2,1,0:T(8,128)S(1)} %pad_maximum_fusion.6), channel_id=1, source_target_pairs={{0,4},{8,0},{16,8},{24,16},{28,24},{20,28},{12,20},{4,12},{1,5},{9... | collective-permute-start | bytes 92168 | tf_op jit(solution)/shard_map/ppermute | solution.py:163
  324.3 20.3 %collective-permute-start.3 = (f32[2,10,384]{2,1,0:T(8,128)S(1)}, f32[2,10,384]{2,1,0:T(8,128)S(1)}, u32[]{:S(2)}, u32[]{:S(2)}) collective-permute-start(f32[2,10,384]{2,1,0:T(8,128)S(1)} %pad_maximum_fusion), channel_id=1, source_target_pairs={{0,8},{8,16},{16,24},{24,28},{28,20},{20,12},{12,4},{4,0},{1,9},{9... | collective-permute-start | bytes 92168 | tf_op jit(solution)/shard_map/ppermute | solution.py:162
  342.4 39.4 %collective-permute-start.19 = (f32[2,10,384]{2,1,0:T(8,128)}, f32[2,10,384]{2,1,0:T(8,128)}, u32[]{:S(2)}, u32[]{:S(2)}) collective-permute-start(f32[2,10,384]{2,1,0:T(8,128)} %pad_maximum_fusion.7), channel_id=1, source_target_pairs={{0,4},{8,0},{16,8},{24,16},{28,24},{20,28},{12,20},{4,12},{1,5},{9... | collective-permute-start | bytes 92168 | tf_op jit(solution)/shard_map/ppermute | solution.py:163
  380.4 4.3 collective-permute-start.5
  383.1 12.7 %collective-permute-start.21 = (f32[2,10,384]{2,1,0:T(8,128)}, f32[2,10,384]{2,1,0:T(8,128)S(1)}, u32[]{:S(2)}, u32[]{:S(2)}) collective-permute-start(f32[2,10,384]{2,1,0:T(8,128)} %pad_maximum_fusion.8), channel_id=1, source_target_pairs={{0,4},{8,0},{16,8},{24,16},{28,24},{20,28},{12,20},{4,12},{1,5},{9... | collective-permute-start | bytes 92168 | tf_op jit(solution)/shard_map/ppermute | solution.py:163
  394.5 4.3 collective-permute-start.7
  396.5 50.1 %collective-permute-start.23 = (f32[2,10,384]{2,1,0:T(8,128)}, f32[2,10,384]{2,1,0:T(8,128)S(1)}, u32[]{:S(2)}, u32[]{:S(2)}) collective-permute-start(f32[2,10,384]{2,1,0:T(8,128)} %pad_maximum_fusion.9), channel_id=1, source_target_pairs={{0,4},{8,0},{16,8},{24,16},{28,24},{20,28},{12,20},{4,12},{1,5},{9... | collective-permute-start | bytes 92168 | tf_op jit(solution)/shard_map/ppermute | solution.py:163
  420.5 21.4 %collective-permute-start.16 = (bf16[384,1280]{1,0:T(8,128)(2,1)S(1)}, bf16[384,1280]{1,0:T(8,128)(2,1)S(1)}, u32[]{:S(2)}, u32[]{:S(2)}) collective-permute-start(bf16[384,1280]{1,0:T(8,128)(2,1)S(1)} %add_convert_fusion.5), channel_id=1, source_target_pairs={{0,4},{8,0},{16,8},{24,16},{28,24},{20,28},{12,20},{4,12},{1,5},{9... | collective-permute-start | bytes 2949128 | tf_op jit(solution)/shard_map/ppermute | solution.py:163
  422.3 21.6 %collective-permute-start.2 = (bf16[384,1280]{1,0:T(8,128)(2,1)S(1)}, bf16[384,1280]{1,0:T(8,128)(2,1)S(1)}, u32[]{:S(2)}, u32[]{:S(2)}) collective-permute-start(bf16[384,1280]{1,0:T(8,128)(2,1)S(1)} %add_convert_fusion.11), channel_id=1, source_target_pairs={{0,8},{8,16},{16,24},{24,28},{28,20},{20,12},{12,4},{4,0},{1,9},{9... | collective-permute-start | bytes 2949128 | tf_op jit(solution)/shard_map/ppermute | solution.py:162
  424.3 63.0 %collective-permute-start.9 = (f32[2,10,384]{2,1,0:T(8,128)}, f32[2,10,384]{2,1,0:T(8,128)S(1)}, u32[]{:S(2)}, u32[]{:S(2)}) collective-permute-start(f32[2,10,384]{2,1,0:T(8,128)} %pad_maximum_fusion.3), channel_id=1, source_target_pairs={{0,8},{8,16},{16,24},{24,28},{28,20},{20,12},{12,4},{4,0},{1,9},{9... | collective-permute-start | bytes 92168 | tf_op jit(solution)/shard_map/ppermute | solution.py:162
  442.4 21.4 %collective-permute-start.18 = (bf16[384,1280]{1,0:T(8,128)(2,1)S(1)}, bf16[384,1280]{1,0:T(8,128)(2,1)S(1)}, u32[]{:S(2)}, u32[]{:S(2)}) collective-permute-start(bf16[384,1280]{1,0:T(8,128)(2,1)S(1)} %add_convert_fusion.4), channel_id=1, source_target_pairs={{0,4},{8,0},{16,8},{24,16},{28,24},{20,28},{12,20},{4,12},{1,5},{9... | collective-permute-start | bytes 2949128 | tf_op jit(solution)/shard_map/ppermute | solution.py:163
  445.1 20.3 %collective-permute-start.4 = (bf16[384,1280]{1,0:T(8,128)(2,1)S(1)}, bf16[384,1280]{1,0:T(8,128)(2,1)S(1)}, u32[]{:S(2)}, u32[]{:S(2)}) collective-permute-start(bf16[384,1280]{1,0:T(8,128)(2,1)S(1)} %add_convert_fusion.10), channel_id=1, source_target_pairs={{0,8},{8,16},{16,24},{24,28},{28,20},{20,12},{12,4},{4,0},{1,9},{9... | collective-permute-start | bytes 2949128 | tf_op jit(solution)/shard_map/ppermute | solution.py:162
  464.2 31.5 %collective-permute-start.20 = (bf16[384,1280]{1,0:T(8,128)(2,1)S(1)}, bf16[384,1280]{1,0:T(8,128)(2,1)}, u32[]{:S(2)}, u32[]{:S(2)}) collective-permute-start(bf16[384,1280]{1,0:T(8,128)(2,1)S(1)} %add_convert_fusion.3), channel_id=1, source_target_pairs={{0,4},{8,0},{16,8},{24,16},{28,24},{20,28},{12,20},{4,12},{1,5},{9... | collective-permute-start | bytes 2949128 | tf_op jit(solution)/shard_map/ppermute | solution.py:163
  467.9 32.3 %collective-permute-start.6 = (bf16[384,1280]{1,0:T(8,128)(2,1)}, bf16[384,1280]{1,0:T(8,128)(2,1)}, u32[]{:S(2)}, u32[]{:S(2)}) collective-permute-start(bf16[384,1280]{1,0:T(8,128)(2,1)} %add_convert_fusion.9), channel_id=1, source_target_pairs={{0,8},{8,16},{16,24},{24,28},{28,20},{20,12},{12,4},{4,0},{1,9},{9... | collective-permute-start | bytes 2949128 | tf_op jit(solution)/shard_map/ppermute | solution.py:162
  486.5 38.7 %collective-permute-start.25 = (f32[2,10,384]{2,1,0:T(8,128)S(1)}, f32[2,10,384]{2,1,0:T(8,128)S(1)}, u32[]{:S(2)}, u32[]{:S(2)}) collective-permute-start(f32[2,10,384]{2,1,0:T(8,128)S(1)} %pad_maximum_fusion.10), channel_id=1, source_target_pairs={{0,4},{8,0},{16,8},{24,16},{28,24},{20,28},{12,20},{4,12},{1,5},{9... | collective-permute-start | bytes 92168 | tf_op jit(solution)/shard_map/ppermute | solution.py:163
  499.0 21.5 %collective-permute-start.22 = (bf16[384,1280]{1,0:T(8,128)(2,1)S(1)}, bf16[384,1280]{1,0:T(8,128)(2,1)S(1)}, u32[]{:S(2)}, u32[]{:S(2)}) collective-permute-start(bf16[384,1280]{1,0:T(8,128)(2,1)S(1)} %add_convert_fusion.2), channel_id=1, source_target_pairs={{0,4},{8,0},{16,8},{24,16},{28,24},{20,28},{12,20},{4,12},{1,5},{9... | collective-permute-start | bytes 2949128 | tf_op jit(solution)/shard_map/ppermute | solution.py:163
  502.1 21.5 %collective-permute-start.8 = (bf16[384,1280]{1,0:T(8,128)(2,1)S(1)}, bf16[384,1280]{1,0:T(8,128)(2,1)S(1)}, u32[]{:S(2)}, u32[]{:S(2)}) collective-permute-start(bf16[384,1280]{1,0:T(8,128)(2,1)S(1)} %add_convert_fusion.8), channel_id=1, source_target_pairs={{0,8},{8,16},{16,24},{24,28},{28,20},{20,12},{12,4},{4,0},{1,9},{9... | collective-permute-start | bytes 2949128 | tf_op jit(solution)/shard_map/ppermute | solution.py:162
  503.6 30.2 %collective-permute-start.11 = (f32[2,10,384]{2,1,0:T(8,128)S(1)}, f32[2,10,384]{2,1,0:T(8,128)S(1)}, u32[]{:S(2)}, u32[]{:S(2)}) collective-permute-start(f32[2,10,384]{2,1,0:T(8,128)S(1)} %pad_maximum_fusion.4), channel_id=1, source_target_pairs={{0,8},{8,16},{16,24},{24,28},{28,20},{20,12},{12,4},{4,0},{1,9},{9... | collective-permute-start | bytes 92168 | tf_op jit(solution)/shard_map/ppermute | solution.py:162
  520.9 21.5 %collective-permute-start.24 = (bf16[384,1280]{1,0:T(8,128)(2,1)S(1)}, bf16[384,1280]{1,0:T(8,128)(2,1)}, u32[]{:S(2)}, u32[]{:S(2)}) collective-permute-start(bf16[384,1280]{1,0:T(8,128)(2,1)S(1)} %add_convert_fusion.1), channel_id=1, source_target_pairs={{0,4},{8,0},{16,8},{24,16},{28,24},{20,28},{12,20},{4,12},{1,5},{9... | collective-permute-start | bytes 2949128 | tf_op jit(solution)/shard_map/ppermute | solution.py:163
  524.9 22.6 %collective-permute-start.10 = (bf16[384,1280]{1,0:T(8,128)(2,1)}, bf16[384,1280]{1,0:T(8,128)(2,1)}, u32[]{:S(2)}, u32[]{:S(2)}) collective-permute-start(bf16[384,1280]{1,0:T(8,128)(2,1)} %add_convert_fusion.7), channel_id=1, source_target_pairs={{0,8},{8,16},{16,24},{24,28},{28,20},{20,12},{12,4},{4,0},{1,9},{9... | collective-permute-start | bytes 2949128 | tf_op jit(solution)/shard_map/ppermute | solution.py:162
  545.7 37.5 %collective-permute-start.26 = (bf16[384,1280]{1,0:T(8,128)(2,1)S(1)}, bf16[384,1280]{1,0:T(8,128)(2,1)}, u32[]{:S(2)}, u32[]{:S(2)}) collective-permute-start(bf16[384,1280]{1,0:T(8,128)(2,1)S(1)} %add_convert_fusion), channel_id=1, source_target_pairs={{0,4},{8,0},{16,8},{24,16},{28,24},{20,28},{12,20},{4,12},{1,5},{9... | collective-permute-start | bytes 2949128 | tf_op jit(solution)/shard_map/ppermute | solution.py:163
  550.1 33.1 %collective-permute-start.12 = (bf16[384,1280]{1,0:T(8,128)(2,1)}, bf16[384,1280]{1,0:T(8,128)(2,1)}, u32[]{:S(2)}, u32[]{:S(2)}) collective-permute-start(bf16[384,1280]{1,0:T(8,128)(2,1)} %add_convert_fusion.6), channel_id=1, source_target_pairs={{0,8},{8,16},{16,24},{24,28},{28,20},{20,12},{12,4},{4,0},{1,9},{9... | collective-permute-start | bytes 2949128 | tf_op jit(solution)/shard_map/ppermute | solution.py:162
  551.0 10.6 %collective-permute-start.27 = (f32[2,10,384]{2,1,0:T(8,128)S(1)}, f32[2,10,384]{2,1,0:T(8,128)S(1)}, u32[]{:S(2)}, u32[]{:S(2)}) collective-permute-start(f32[2,10,384]{2,1,0:T(8,128)S(1)} %pad_maximum_fusion.11), channel_id=1, source_target_pairs={{0,4},{8,0},{16,8},{24,16},{28,24},{20,28},{12,20},{4,12},{1,5},{9... | collective-permute-start | bytes 92168 | tf_op jit(solution)/shard_map/ppermute | solution.py:163
  552.2 13.7 %collective-permute-start.13 = (f32[2,10,384]{2,1,0:T(8,128)S(1)}, f32[2,10,384]{2,1,0:T(8,128)S(1)}, u32[]{:S(2)}, u32[]{:S(2)}) collective-permute-start(f32[2,10,384]{2,1,0:T(8,128)S(1)} %pad_maximum_fusion.5), channel_id=1, source_target_pairs={{0,8},{8,16},{16,24},{24,28},{28,20},{20,12},{12,4},{4,0},{1,9},{9... | collective-permute-start | bytes 92168 | tf_op jit(solution)/shard_map/ppermute | solution.py:162
  (50 other events, 394.1 us)
Sparse Core Ops, SparseCore 0:
  9.5 217.2 all-gather.2
  614.2 51.0 reduce-scatter.1

commit v4 on v3

v4 whole, which is shorter than its diff:
```python
import jax
import jax.numpy as jnp
from jax import lax
from jax.experimental import pallas as pl
from jax.experimental.pallas import tpu as pltpu
from jax.sharding import PartitionSpec as P

HD = 128
TILE = 128


NEG = -1e30


def _scores(q_ref, kf0_ref, kf1_ref, ks_ref, j, second, valid):
    sl = slice(j * HD, (j + 1) * HD)
    qj = q_ref[0, :, sl]
    dims = (((1,), (1,)), ((), ()))
    scale = HD ** -0.5
    s0 = lax.dot_general(kf0_ref[0, :, sl], qj, dims, preferred_element_type=jnp.float32) * scale
    s1 = lax.dot_general(kf1_ref[0, :, sl], qj, dims, preferred_element_type=jnp.float32) * scale
    s2 = lax.dot_general(ks_ref[0, :, sl], qj, dims, preferred_element_type=jnp.float32) * scale
    s1 = jnp.where(second > 0, s1, NEG)
    s2 = jnp.where(valid > 0, s2, NEG)
    return s0, s1, s2


def acc_kernel(
    fsel_ref, sidx_ref, sval_ref, fslot_ref, bslot_ref,
    q_ref, kf0_ref, kf1_ref, ks_ref, vf0_ref, vf1_ref, vs_ref,
    accf_ref, accb_ref, stf_ref, stb_ref,
):
    r = pl.program_id(0)
    heads_here = q_ref.shape[2] // HD
    split = accf_ref.shape[1] // HD
    second = fsel_ref[2]
    valid = sval_ref[r]
    tn = (((0,), (0,)), ((), ()))
    for j in range(heads_here):
        sl = slice(j * HD, (j + 1) * HD)
        s0, s1, s2 = _scores(q_ref, kf0_ref, kf1_ref, ks_ref, j, second, valid)
        top = jnp.maximum(
            jnp.maximum(jnp.max(s0, axis=0, keepdims=True), jnp.max(s1, axis=0, keepdims=True)),
            jnp.max(s2, axis=0, keepdims=True),
        )
        w0 = jnp.exp(s0 - top)
        w1 = jnp.exp(s1 - top)
        w2 = jnp.exp(s2 - top)
        total = (
            jnp.sum(w0, axis=0, keepdims=True)
            + jnp.sum(w1, axis=0, keepdims=True)
            + jnp.sum(w2, axis=0, keepdims=True)
        )
        summed = (
            lax.dot_general(vf0_ref[0, :, sl], w0.astype(jnp.bfloat16), tn, preferred_element_type=jnp.float32)
            + lax.dot_general(vf1_ref[0, :, sl], w1.astype(jnp.bfloat16), tn, preferred_element_type=jnp.float32)
            + lax.dot_general(vs_ref[0, :, sl], w2.astype(jnp.bfloat16), tn, preferred_element_type=jnp.float32)
        )
        if j < split:
            accf_ref[0, sl, :] = summed.astype(accf_ref.dtype)
            stf_ref[0, 0, j : j + 1, :] = top
            stf_ref[0, 1, j : j + 1, :] = total
        else:
            i = j - split
            accb_ref[0, i * HD : (i + 1) * HD, :] = summed.astype(accb_ref.dtype)
            stb_ref[0, 0, i : i + 1, :] = top
            stb_ref[0, 1, i : i + 1, :] = total


def ring_order(n):
    if n == 8:
        return [0, 2, 4, 6, 7, 5, 3, 1]
    return list(range(n))


def combine(run, mine):
    acc_r, stat_r = run
    acc_o, stat_o = mine
    top = jnp.maximum(stat_r[0], stat_o[0])
    f_r = jnp.exp(stat_r[0] - top)
    f_o = jnp.exp(stat_o[0] - top)
    total = stat_r[1] * f_r + stat_o[1] * f_o
    acc = acc_r.astype(jnp.float32) * jnp.repeat(f_r, HD, axis=0) + acc_o.astype(
        jnp.float32
    ) * jnp.repeat(f_o, HD, axis=0)
    return acc, jnp.stack([top, total])


def on_device(
    queries,
    fresh_key,
    fresh_value,
    stale_key,
    stale_value,
    slot_tiles,
    refresh,
    stale_reads,
    out_weight,
):
    tokens_here = queries.shape[0]
    width_here = queries.shape[1]
    heads_here = width_here // HD
    tile_dev = tokens_here // TILE
    readers = stale_reads.shape[0]
    me = lax.axis_index("seq")

    my_refresh = lax.dynamic_slice_in_dim(refresh, me * tile_dev, tile_dev, 0)
    first = jnp.argmax(my_refresh).astype(jnp.int32)
    last = (tile_dev - 1 - jnp.argmax(my_refresh[::-1])).astype(jnp.int32)
    second = (jnp.sum(my_refresh) >= 2).astype(jnp.int32)
    fsel = jnp.stack([first, last, second])

    my_slots = lax.dynamic_slice_in_dim(slot_tiles, me * tile_dev, tile_dev, 0)
    wanted = jnp.take(stale_reads, my_slots, axis=1)
    sidx = jnp.argmax(wanted, axis=1).astype(jnp.int32)
    sval = jnp.max(wanted, axis=1).astype(jnp.int32)

    q_all = lax.all_gather(queries, "seq", axis=0, tiled=False)
    fk3 = fresh_key.reshape(tile_dev, TILE, width_here)
    fv3 = fresh_value.reshape(tile_dev, TILE, width_here)
    sk3 = stale_key.reshape(tile_dev, TILE, width_here)
    sv3 = stale_value.reshape(tile_dev, TILE, width_here)

    ring = ring_order(readers)
    place = [0] * readers
    for i, d in enumerate(ring):
        place[d] = i
    pos = jnp.array(place, jnp.int32)[me]
    place_arr = jnp.array(place, jnp.int32)
    fslot = (pos - 1 - place_arr + readers) % readers
    bslot = (place_arr - pos - 1 + 2 * readers) % readers
    forward = [(ring[i], ring[(i + 1) % readers]) for i in range(readers)]
    backward = [(ring[i], ring[(i - 1) % readers]) for i in range(readers)]
    split = heads_here // 2
    rest = heads_here - split

    q_spec = pl.BlockSpec((1, tokens_here, width_here), lambda r, f, s, v, a, b: (r, 0, 0))
    f0_spec = pl.BlockSpec((1, TILE, width_here), lambda r, f, s, v, a, b: (f[0], 0, 0))
    f1_spec = pl.BlockSpec((1, TILE, width_here), lambda r, f, s, v, a, b: (f[1], 0, 0))
    s_spec = pl.BlockSpec((1, TILE, width_here), lambda r, f, s, v, a, b: (s[r], 0, 0))
    accf_spec = pl.BlockSpec((1, split * HD, tokens_here), lambda r, f, s, v, a, b: (a[r], 0, 0))
    accb_spec = pl.BlockSpec((1, rest * HD, tokens_here), lambda r, f, s, v, a, b: (b[r], 0, 0))
    stf_spec = pl.BlockSpec((1, 2, split, tokens_here), lambda r, f, s, v, a, b: (a[r], 0, 0, 0))
    stb_spec = pl.BlockSpec((1, 2, rest, tokens_here), lambda r, f, s, v, a, b: (b[r], 0, 0, 0))
    params = pltpu.CompilerParams(dimension_semantics=("arbitrary",))

    acc_f, acc_b, st_f, st_b = pl.pallas_call(
        acc_kernel,
        grid_spec=pltpu.PrefetchScalarGridSpec(
            num_scalar_prefetch=5,
            grid=(readers,),
            in_specs=[q_spec, f0_spec, f1_spec, s_spec, f0_spec, f1_spec, s_spec],
            out_specs=[accf_spec, accb_spec, stf_spec, stb_spec],
        ),
        out_shape=[
            jax.ShapeDtypeStruct((readers, split * HD, tokens_here), jnp.bfloat16),
            jax.ShapeDtypeStruct((readers, rest * HD, tokens_here), jnp.bfloat16),
            jax.ShapeDtypeStruct((readers, 2, split, tokens_here), jnp.float32),
            jax.ShapeDtypeStruct((readers, 2, rest, tokens_here), jnp.float32),
        ],
        compiler_params=params,
    )(fsel, sidx, sval, fslot, bslot, q_all, fk3, fk3, sk3, fv3, fv3, sv3)

    run_f = (acc_f[0], st_f[0])
    run_b = (acc_b[0], st_b[0])
    for k in range(1, readers):
        got_f = lax.ppermute(run_f, "seq", forward)
        got_b = lax.ppermute(run_b, "seq", backward)
        run_f = combine(got_f, (acc_f[k], st_f[k]))
        run_b = combine(got_b, (acc_b[k], st_b[k]))
        if k < readers - 1:
            run_f = (run_f[0].astype(jnp.bfloat16), run_f[1])
            run_b = (run_b[0].astype(jnp.bfloat16), run_b[1])
    acc = jnp.concatenate([run_f[0], run_b[0]], axis=0)
    total = jnp.concatenate([run_f[1][1], run_b[1][1]], axis=0)
    attended = (acc / jnp.repeat(total, HD, axis=0)).astype(jnp.bfloat16)
    mixed = lax.dot_general(
        attended, out_weight, (((0,), (0,)), ((), ())), preferred_element_type=jnp.float32
    )
    return lax.psum_scatter(mixed.astype(jnp.bfloat16), "head", scatter_dimension=0, tiled=True)


def solution(mesh):
    return jax.shard_map(
        on_device,
        mesh=mesh,
        in_specs=(
            P(("cfg", "seq"), "head"),
            P(("cfg", "seq"), "head"),
            P(("cfg", "seq"), "head"),
            P(("cfg", "seq"), "head"),
            P(("cfg", "seq"), "head"),
            P("cfg"),
            P("cfg"),
            P("cfg", None),
            P("head", None),
        ),
        out_specs=P(("cfg", "seq", "head"), None),
        check_vma=False,
    )
```

time: 681 us -> 545 us (0.80); the launches traced: 673 us -> 544 us
  local copies, waits for them, and re-layouts: 151 us -> 6.58 us
  waiting for transfers between devices: 311 us -> 389 us
  between operations: 51 us -> 15.8 us
  other arithmetic: 45.7 us -> 14.4 us
    mul x56 -> x0, local copies, waits for them, and re-layouts: 120 us -> none  [the longest x28 60.1 us: combine(): acc_o.astype(jnp.float32).reshape(tokens, hh, HD) * f_o.T[:, :, None]]
    all_gather x1, waiting for transfers between devices: 176 us -> 210 us  [on_device(): q_all = lax.all_gather(queries, 'seq', axis=0, tiled=False)]
    ppermute x14, waiting for transfers between devices: 74.4 us -> 102 us  [on_device(): got_b = lax.ppermute(run_b, 'seq', backward)]
    ppermute x14, waiting for transfers between devices: 8.26 us -> 25.6 us  [on_device(): got_f = lax.ppermute(run_f, 'seq', forward)]
    squeeze x1 -> x4, local copies, waits for them, and re-layouts: 17.3 us -> 5.16 us  [the longest x2 2.85 us: on_device(): run_b = (acc_b[0], st_b[0])]
  transfers between devices with their start and end apart: 30 -> 30, of which waited for: 13 -> 13; matrix products, arithmetic and copies ran while one was open for 26% -> 3% of each run, Pallas kernels for 0% -> 0%
where the time goes in v4:
time: 545 us; the launch traced here: 544 us
  waiting for transfers between devices  389 us (71%)
  Pallas kernels  72 us (13%)
  starting transfers between devices  29 us (5%)
  matrix products  16.8 us (3%)
  between operations  15.8 us (3%)
  other arithmetic  14.4 us (3%)
  local copies, waits for them, and re-layouts  6.58 us (1%)
    all_gather x1, waiting for transfers between devices, on_device(): q_all = lax.all_gather(queries, 'seq', axis=0, tiled=False)  210 us
    ppermute x14, waiting for transfers between devices, on_device(): got_b = lax.ppermute(run_b, 'seq', backward)  102 us
    pallas_call x1, Pallas kernels, on_device(): pl.pallas_call(acc_kernel, grid_spec=pltpu.PrefetchScalarGridSpec(num_sca...  72 us
    reduce_scatter x1, waiting for transfers between devices, on_device(): lax.psum_scatter(mixed.astype(jnp.bfloat16), 'head', scatter_dimension=0,...  50.7 us
    ppermute x14, waiting for transfers between devices, on_device(): got_f = lax.ppermute(run_f, 'seq', forward)  25.6 us
    dot_general x1, matrix products, on_device(): lax.dot_general(attended, out_weight, (((0,), (0,)), ((), ())), preferred...  16.8 us
    ppermute x14, starting transfers between devices, on_device(): got_b = lax.ppermute(run_b, 'seq', backward)  16.8 us
    ppermute x14, starting transfers between devices, on_device(): got_f = lax.ppermute(run_f, 'seq', forward)  12.1 us
  transfers between devices with their start and end apart: 30, of which 13 were waited for; matrix products, arithmetic and copies ran while one was open for 3% of the time, Pallas kernels for 0%

profile of v4, /device:TPU:0, one launch (start us, length us, event | category | flops | bytes accessed | tf_op | source)
XLA Modules:
  0.0 543.9 jit_solution(12432483231454750344)
XLA Ops:
  13.0 1.2 pad_add_fusion.fsel_ref
  14.8 1.2 and_select_fusion
  16.7 210.1 %all-gather.3.cloned.1.call-done = bf16[3072,2560]{1,0:T(8,128)(2,1)} async-done(((bf16[384,2560]{1,0:T(8,128)(2,1)}), bf16[3072,2560]{1,0:T(8,128)(2,1)}) %all-gather.3.cloned.1.call-update) | async-done | bytes 15728656 | tf_op jit(solution)/shard_map/all_gather | solution.py:118
  226.8 72.0 %shard_map.109 = (bf16[8,1280,384]{2,1,0:T(8,128)(2,1)}, bf16[8,1280,384]{2,1,0:T(8,128)(2,1)}, f32[8,2,10,384]{3,2,1,0:T(8,128)}, f32[8,2,10,384]{3,2,1,0:T(8,128)}) custom-call(s32[3]{0:T(128)} %pad_add_fusion.fsel_ref, s32[8]{0:T(128)} %get-tuple-element.14.sidx_ref, s32[8]{0:T(128)} %select_reduce_fusion.sval_ref, s32[8]{0:T(128)} %get-tuple-element.98.fslot_ref, ...), custom_call_target="tpu_custom_call" | custom-call | tf_op jit(solution)/shard_map/pallas_call | solution.py:147
  302.4 1.4 slice_bitcast_fusion.1
  303.9 2.0 slice_bitcast_fusion
  305.9 1.2 collective-permute-start.14
  308.1 1.2 collective-permute-start.17
  310.2 19.5 %collective-permute-done.17 = f32[2,10,384]{2,1,0:T(8,128)S(1)} collective-permute-done((f32[2,10,384]{2,1,0:T(8,128)S(1)}, f32[2,10,384]{2,1,0:T(8,128)S(1)}, u32[]{:S(2)}, u32[]{:S(2)}) %collective-permute-start.17) | collective-permute-done | bytes 30752 | tf_op jit(solution)/shard_map/ppermute | solution.py:168
  330.6 1.4 collective-permute-start.5
  331.9 2.0 collective-permute-done.19
  334.8 1.6 fusion.13
  337.2 1.7 collective-permute-start.2
  339.4 1.7 collective-permute-start.7
  341.1 16.9 %collective-permute-done.21 = f32[2,10,384]{2,1,0:T(8,128)S(1)} collective-permute-done((f32[2,10,384]{2,1,0:T(8,128)S(1)}, f32[2,10,384]{2,1,0:T(8,128)S(1)}, u32[]{:S(2)}, u32[]{:S(2)}) %collective-permute-start.21) | collective-permute-done | bytes 30752 | tf_op jit(solution)/shard_map/ppermute | solution.py:168
  359.0 1.6 fusion.11
  360.6 1.9 collective-permute-start.18
  364.4 1.2 collective-permute-start.25
  365.6 19.0 %collective-permute-done.9 = f32[2,10,384]{2,1,0:T(8,128)S(1)} collective-permute-done((f32[2,10,384]{2,1,0:T(8,128)S(1)}, f32[2,10,384]{2,1,0:T(8,128)S(1)}, u32[]{:S(2)}, u32[]{:S(2)}) %collective-permute-start.9) | collective-permute-done | bytes 30752 | tf_op jit(solution)/shard_map/ppermute | solution.py:167
  385.2 1.9 collective-permute-start.20
  387.8 1.9 collective-permute-start.27
  390.0 15.8 %collective-permute-done.27 = f32[2,10,384]{2,1,0:T(8,128)S(1)} collective-permute-done((f32[2,10,384]{2,1,0:T(8,128)S(1)}, f32[2,10,384]{2,1,0:T(8,128)S(1)}, u32[]{:S(2)}, u32[]{:S(2)}) %collective-permute-start.27) | collective-permute-done | bytes 30752 | tf_op jit(solution)/shard_map/ppermute | solution.py:168
  405.8 3.7 collective-permute-done.13
  410.4 2.1 collective-permute-start.8
  412.4 17.4 %collective-permute-done.22 = bf16[1280,384]{1,0:T(8,128)(2,1)S(1)} collective-permute-done((bf16[1280,384]{1,0:T(8,128)(2,1)S(1)}, bf16[1280,384]{1,0:T(8,128)(2,1)S(1)}, u32[]{:S(2)}, u32[]{:S(2)}) %collective-permute-start.22) | collective-permute-done | bytes 983072 | tf_op jit(solution)/shard_map/ppermute | solution.py:168
  430.2 1.7 collective-permute-start.24
  432.7 19.0 %collective-permute-done.24 = bf16[1280,384]{1,0:T(8,128)(2,1)S(1)} collective-permute-done((bf16[1280,384]{1,0:T(8,128)(2,1)S(1)}, bf16[1280,384]{1,0:T(8,128)(2,1)S(1)}, u32[]{:S(2)}, u32[]{:S(2)}) %collective-permute-start.24) | collective-permute-done | bytes 983072 | tf_op jit(solution)/shard_map/ppermute | solution.py:168
  452.1 1.7 collective-permute-start.26
  454.7 11.8 %collective-permute-done.26 = bf16[1280,384]{1,0:T(8,128)(2,1)S(1)} collective-permute-done((bf16[1280,384]{1,0:T(8,128)(2,1)S(1)}, bf16[1280,384]{1,0:T(8,128)(2,1)S(1)}, u32[]{:S(2)}, u32[]{:S(2)}) %collective-permute-start.26) | collective-permute-done | bytes 983072 | tf_op jit(solution)/shard_map/ppermute | solution.py:168
  466.8 2.1 collective-permute-done.12
  469.6 16.8 %convolution_convert_fusion = bf16[384,5120]{1,0:T(8,128)(2,1)} fusion(bf16[2560,384]{1,0:T(8,128)(2,1)S(1)} %fusion, bf16[2560,5120]{1,0:T(8,128)(2,1)} %param.19), kind=kOutput, calls=%fused_computation.1 | convolution fusion | flops 10068295680 | bytes 32112640 | tf_op jit(solution)/shard_map/dot_general | solution.py:177
  486.4 50.7 %reduce-scatter.2.cloned.1.call-done = bf16[192,5120]{1,0:T(8,128)(2,1)} async-done(((bf16[384,5120]{1,0:T(8,128)(2,1)}), bf16[192,5120]{1,0:T(8,128)(2,1)}) %reduce-scatter.2.cloned.1.call-update) | async-done | bytes 1966096 | tf_op jit(solution)/shard_map/reduce_scatter | solution.py:180
  (111 shorter events, 22.8 us)
Async XLA Ops:
  6.5 220.2 %all-gather.3.cloned.1.call-start = ((), (), s32[]{:S(2)}) async-start(), calls=%async_computation.2 | async-start | bytes 17694720 | tf_op jit(solution)/shard_map/all_gather | solution.py:118
  7.3 529.8 %reduce-scatter.2.cloned.1.call-start = ((), (), s32[]{:S(2)}) async-start(), calls=%async_computation.1 | async-start | bytes 5898240 | tf_op jit(solution)/shard_map/reduce_scatter | solution.py:180
  300.4 7.6 %collective-permute-start.15 = (f32[2,10,384]{2,1,0:T(8,128)S(1)}, f32[2,10,384]{2,1,0:T(8,128)S(1)}, u32[]{:S(2)}, u32[]{:S(2)}) collective-permute-start(f32[2,10,384]{2,1,0:T(8,128)S(1)} %slice_bitcast_fusion.2), channel_id=1, source_target_pairs={{0,4},{8,0},{16,8},{24,16},{28,24},{20,28},{12,20},{4,12},{1,5},{9... | collective-permute-start | bytes 92168 | tf_op jit(solution)/shard_map/ppermute | solution.py:168
  301.6 7.7 %collective-permute-start.1 = (f32[2,10,384]{2,1,0:T(8,128)S(1)}, f32[2,10,384]{2,1,0:T(8,128)S(1)}, u32[]{:S(2)}, u32[]{:S(2)}) collective-permute-start(f32[2,10,384]{2,1,0:T(8,128)S(1)} %slice_bitcast_fusion.3), channel_id=1, source_target_pairs={{0,8},{8,16},{16,24},{24,28},{28,20},{20,12},{12,4},{4,0},{1,9},{9... | collective-permute-start | bytes 92168 | tf_op jit(solution)/shard_map/ppermute | solution.py:167
  302.4 34.4 %copy-start = (bf16[8,1280,384]{2,1,0:T(8,128)(2,1)S(1)}, bf16[8,1280,384]{2,1,0:T(8,128)(2,1)}, u32[]{:S(2)}) copy-start(bf16[8,1280,384]{2,1,0:T(8,128)(2,1)} %get-tuple-element.15) | copy-start | bytes 23592964
  305.9 28.8 %collective-permute-start.14 = (bf16[1280,384]{1,0:T(8,128)(2,1)S(1)}, bf16[1280,384]{1,0:T(8,128)(2,1)S(1)}, u32[]{:S(2)}, u32[]{:S(2)}) collective-permute-start(bf16[1280,384]{1,0:T(8,128)(2,1)S(1)} %slice_bitcast_fusion), channel_id=1, source_target_pairs={{0,4},{8,0},{16,8},{24,16},{28,24},{20,28},{12,20},{4,12},{1,5},{9... | collective-permute-start | bytes 2949128 | tf_op jit(solution)/shard_map/ppermute | solution.py:168
  307.2 29.7 %collective-permute-start = (bf16[1280,384]{1,0:T(8,128)(2,1)S(1)}, bf16[1280,384]{1,0:T(8,128)(2,1)S(1)}, u32[]{:S(2)}, u32[]{:S(2)}) collective-permute-start(bf16[1280,384]{1,0:T(8,128)(2,1)S(1)} %slice_bitcast_fusion.1), channel_id=1, source_target_pairs={{0,8},{8,16},{16,24},{24,28},{28,20},{20,12},{12,4},{4,0},{1,9},{9... | collective-permute-start | bytes 2949128 | tf_op jit(solution)/shard_map/ppermute | solution.py:167
  308.1 21.7 %collective-permute-start.17 = (f32[2,10,384]{2,1,0:T(8,128)S(1)}, f32[2,10,384]{2,1,0:T(8,128)S(1)}, u32[]{:S(2)}, u32[]{:S(2)}) collective-permute-start(f32[2,10,384]{2,1,0:T(8,128)S(1)} %pad_maximum_fusion.6), channel_id=1, source_target_pairs={{0,4},{8,0},{16,8},{24,16},{28,24},{20,28},{12,20},{4,12},{1,5},{9... | collective-permute-start | bytes 92168 | tf_op jit(solution)/shard_map/ppermute | solution.py:168
  309.3 21.2 %collective-permute-start.3 = (f32[2,10,384]{2,1,0:T(8,128)S(1)}, f32[2,10,384]{2,1,0:T(8,128)S(1)}, u32[]{:S(2)}, u32[]{:S(2)}) collective-permute-start(f32[2,10,384]{2,1,0:T(8,128)S(1)} %pad_maximum_fusion), channel_id=1, source_target_pairs={{0,8},{8,16},{16,24},{24,28},{28,20},{20,12},{12,4},{4,0},{1,9},{9... | collective-permute-start | bytes 92168 | tf_op jit(solution)/shard_map/ppermute | solution.py:167
  329.8 4.1 collective-permute-start.19
  330.6 4.1 collective-permute-start.5
  336.4 22.7 %collective-permute-start.16 = (bf16[1280,384]{1,0:T(8,128)(2,1)S(1)}, bf16[1280,384]{1,0:T(8,128)(2,1)S(1)}, u32[]{:S(2)}, u32[]{:S(2)}) collective-permute-start(bf16[1280,384]{1,0:T(8,128)(2,1)S(1)} %fusion.13), channel_id=1, source_target_pairs={{0,4},{8,0},{16,8},{24,16},{28,24},{20,28},{12,20},{4,12},{1,5},{9... | collective-permute-start | bytes 2949128 | tf_op jit(solution)/shard_map/ppermute | solution.py:168
  336.8 48.0 %copy-start.1 = (bf16[8,1280,384]{2,1,0:T(8,128)(2,1)S(1)}, bf16[8,1280,384]{2,1,0:T(8,128)(2,1)}, u32[]{:S(2)}) copy-start(bf16[8,1280,384]{2,1,0:T(8,128)(2,1)} %get-tuple-element.17) | copy-start | bytes 23592964
  337.2 25.4 %collective-permute-start.2 = (bf16[1280,384]{1,0:T(8,128)(2,1)S(1)}, bf16[1280,384]{1,0:T(8,128)(2,1)S(1)}, u32[]{:S(2)}, u32[]{:S(2)}) collective-permute-start(bf16[1280,384]{1,0:T(8,128)(2,1)S(1)} %fusion.26), channel_id=1, source_target_pairs={{0,8},{8,16},{16,24},{24,28},{28,20},{20,12},{12,4},{4,0},{1,9},{9... | collective-permute-start | bytes 2949128 | tf_op jit(solution)/shard_map/ppermute | solution.py:167
  338.9 19.0 %collective-permute-start.21 = (f32[2,10,384]{2,1,0:T(8,128)S(1)}, f32[2,10,384]{2,1,0:T(8,128)S(1)}, u32[]{:S(2)}, u32[]{:S(2)}) collective-permute-start(f32[2,10,384]{2,1,0:T(8,128)S(1)} %pad_maximum_fusion.8), channel_id=1, source_target_pairs={{0,4},{8,0},{16,8},{24,16},{28,24},{20,28},{12,20},{4,12},{1,5},{9... | collective-permute-start | bytes 92168 | tf_op jit(solution)/shard_map/ppermute | solution.py:168
  339.4 23.7 %collective-permute-start.7 = (f32[2,10,384]{2,1,0:T(8,128)S(1)}, f32[2,10,384]{2,1,0:T(8,128)S(1)}, u32[]{:S(2)}, u32[]{:S(2)}) collective-permute-start(f32[2,10,384]{2,1,0:T(8,128)S(1)} %pad_maximum_fusion.2), channel_id=1, source_target_pairs={{0,8},{8,16},{16,24},{24,28},{28,20},{20,12},{12,4},{4,0},{1,9},{9... | collective-permute-start | bytes 92168 | tf_op jit(solution)/shard_map/ppermute | solution.py:167
  358.0 6.3 %collective-permute-start.23 = (f32[2,10,384]{2,1,0:T(8,128)S(1)}, f32[2,10,384]{2,1,0:T(8,128)S(1)}, u32[]{:S(2)}, u32[]{:S(2)}) collective-permute-start(f32[2,10,384]{2,1,0:T(8,128)S(1)} %pad_maximum_fusion.9), channel_id=1, source_target_pairs={{0,4},{8,0},{16,8},{24,16},{28,24},{20,28},{12,20},{4,12},{1,5},{9... | collective-permute-start | bytes 92168 | tf_op jit(solution)/shard_map/ppermute | solution.py:168
  360.6 24.2 %collective-permute-start.18 = (bf16[1280,384]{1,0:T(8,128)(2,1)S(1)}, bf16[1280,384]{1,0:T(8,128)(2,1)S(1)}, u32[]{:S(2)}, u32[]{:S(2)}) collective-permute-start(bf16[1280,384]{1,0:T(8,128)(2,1)S(1)} %fusion.11), channel_id=1, source_target_pairs={{0,4},{8,0},{16,8},{24,16},{28,24},{20,28},{12,20},{4,12},{1,5},{9... | collective-permute-start | bytes 2949128 | tf_op jit(solution)/shard_map/ppermute | solution.py:168
  363.0 24.2 %collective-permute-start.4 = (bf16[1280,384]{1,0:T(8,128)(2,1)S(1)}, bf16[1280,384]{1,0:T(8,128)(2,1)S(1)}, u32[]{:S(2)}, u32[]{:S(2)}) collective-permute-start(bf16[1280,384]{1,0:T(8,128)(2,1)S(1)} %fusion.24), channel_id=1, source_target_pairs={{0,8},{8,16},{16,24},{24,28},{28,20},{20,12},{12,4},{4,0},{1,9},{9... | collective-permute-start | bytes 2949128 | tf_op jit(solution)/shard_map/ppermute | solution.py:167
  363.2 21.4 %collective-permute-start.9 = (f32[2,10,384]{2,1,0:T(8,128)S(1)}, f32[2,10,384]{2,1,0:T(8,128)S(1)}, u32[]{:S(2)}, u32[]{:S(2)}) collective-permute-start(f32[2,10,384]{2,1,0:T(8,128)S(1)} %pad_maximum_fusion.3), channel_id=1, source_target_pairs={{0,8},{8,16},{16,24},{24,28},{28,20},{20,12},{12,4},{4,0},{1,9},{9... | collective-permute-start | bytes 92168 | tf_op jit(solution)/shard_map/ppermute | solution.py:167
  364.4 23.4 %collective-permute-start.25 = (f32[2,10,384]{2,1,0:T(8,128)S(1)}, f32[2,10,384]{2,1,0:T(8,128)S(1)}, u32[]{:S(2)}, u32[]{:S(2)}) collective-permute-start(f32[2,10,384]{2,1,0:T(8,128)S(1)} %pad_maximum_fusion.10), channel_id=1, source_target_pairs={{0,4},{8,0},{16,8},{24,16},{28,24},{20,28},{12,20},{4,12},{1,5},{9... | collective-permute-start | bytes 92168 | tf_op jit(solution)/shard_map/ppermute | solution.py:168
  384.6 5.1 collective-permute-start.11
  385.2 24.3 %collective-permute-start.20 = (bf16[1280,384]{1,0:T(8,128)(2,1)S(1)}, bf16[1280,384]{1,0:T(8,128)(2,1)S(1)}, u32[]{:S(2)}, u32[]{:S(2)}) collective-permute-start(bf16[1280,384]{1,0:T(8,128)(2,1)S(1)} %fusion.9), channel_id=1, source_target_pairs={{0,4},{8,0},{16,8},{24,16},{28,24},{20,28},{12,20},{4,12},{1,5},{9... | collective-permute-start | bytes 2949128 | tf_op jit(solution)/shard_map/ppermute | solution.py:168
  387.6 22.4 %collective-permute-start.6 = (bf16[1280,384]{1,0:T(8,128)(2,1)S(1)}, bf16[1280,384]{1,0:T(8,128)(2,1)S(1)}, u32[]{:S(2)}, u32[]{:S(2)}) collective-permute-start(bf16[1280,384]{1,0:T(8,128)(2,1)S(1)} %fusion.22), channel_id=1, source_target_pairs={{0,8},{8,16},{16,24},{24,28},{28,20},{20,12},{12,4},{4,0},{1,9},{9... | collective-permute-start | bytes 2949128 | tf_op jit(solution)/shard_map/ppermute | solution.py:167
  387.8 18.0 %collective-permute-start.27 = (f32[2,10,384]{2,1,0:T(8,128)S(1)}, f32[2,10,384]{2,1,0:T(8,128)S(1)}, u32[]{:S(2)}, u32[]{:S(2)}) collective-permute-start(f32[2,10,384]{2,1,0:T(8,128)S(1)} %pad_maximum_fusion.11), channel_id=1, source_target_pairs={{0,4},{8,0},{16,8},{24,16},{28,24},{20,28},{12,20},{4,12},{1,5},{9... | collective-permute-start | bytes 92168 | tf_op jit(solution)/shard_map/ppermute | solution.py:168
  389.8 19.7 %collective-permute-start.13 = (f32[2,10,384]{2,1,0:T(8,128)S(1)}, f32[2,10,384]{2,1,0:T(8,128)S(1)}, u32[]{:S(2)}, u32[]{:S(2)}) collective-permute-start(f32[2,10,384]{2,1,0:T(8,128)S(1)} %pad_maximum_fusion.5), channel_id=1, source_target_pairs={{0,8},{8,16},{16,24},{24,28},{28,20},{20,12},{12,4},{4,0},{1,9},{9... | collective-permute-start | bytes 92168 | tf_op jit(solution)/shard_map/ppermute | solution.py:167
  409.9 19.9 %collective-permute-start.22 = (bf16[1280,384]{1,0:T(8,128)(2,1)S(1)}, bf16[1280,384]{1,0:T(8,128)(2,1)S(1)}, u32[]{:S(2)}, u32[]{:S(2)}) collective-permute-start(bf16[1280,384]{1,0:T(8,128)(2,1)S(1)} %fusion.7), channel_id=1, source_target_pairs={{0,4},{8,0},{16,8},{24,16},{28,24},{20,28},{12,20},{4,12},{1,5},{9... | collective-permute-start | bytes 2949128 | tf_op jit(solution)/shard_map/ppermute | solution.py:168
  410.4 21.5 %collective-permute-start.8 = (bf16[1280,384]{1,0:T(8,128)(2,1)S(1)}, bf16[1280,384]{1,0:T(8,128)(2,1)S(1)}, u32[]{:S(2)}, u32[]{:S(2)}) collective-permute-start(bf16[1280,384]{1,0:T(8,128)(2,1)S(1)} %fusion.20), channel_id=1, source_target_pairs={{0,8},{8,16},{16,24},{24,28},{28,20},{20,12},{12,4},{4,0},{1,9},{9... | collective-permute-start | bytes 2949128 | tf_op jit(solution)/shard_map/ppermute | solution.py:167
  430.2 21.5 %collective-permute-start.24 = (bf16[1280,384]{1,0:T(8,128)(2,1)S(1)}, bf16[1280,384]{1,0:T(8,128)(2,1)S(1)}, u32[]{:S(2)}, u32[]{:S(2)}) collective-permute-start(bf16[1280,384]{1,0:T(8,128)(2,1)S(1)} %fusion.5), channel_id=1, source_target_pairs={{0,4},{8,0},{16,8},{24,16},{28,24},{20,28},{12,20},{4,12},{1,5},{9... | collective-permute-start | bytes 2949128 | tf_op jit(solution)/shard_map/ppermute | solution.py:168
  432.3 21.5 %collective-permute-start.10 = (bf16[1280,384]{1,0:T(8,128)(2,1)S(1)}, bf16[1280,384]{1,0:T(8,128)(2,1)S(1)}, u32[]{:S(2)}, u32[]{:S(2)}) collective-permute-start(bf16[1280,384]{1,0:T(8,128)(2,1)S(1)} %fusion.18), channel_id=1, source_target_pairs={{0,8},{8,16},{16,24},{24,28},{28,20},{20,12},{12,4},{4,0},{1,9},{9... | collective-permute-start | bytes 2949128 | tf_op jit(solution)/shard_map/ppermute | solution.py:167
  452.1 14.3 %collective-permute-start.26 = (bf16[1280,384]{1,0:T(8,128)(2,1)S(1)}, bf16[1280,384]{1,0:T(8,128)(2,1)S(1)}, u32[]{:S(2)}, u32[]{:S(2)}) collective-permute-start(bf16[1280,384]{1,0:T(8,128)(2,1)S(1)} %fusion.3), channel_id=1, source_target_pairs={{0,4},{8,0},{16,8},{24,16},{28,24},{20,28},{12,20},{4,12},{1,5},{9... | collective-permute-start | bytes 2949128 | tf_op jit(solution)/shard_map/ppermute | solution.py:168
  454.2 14.7 %collective-permute-start.12 = (bf16[1280,384]{1,0:T(8,128)(2,1)S(1)}, bf16[1280,384]{1,0:T(8,128)(2,1)S(1)}, u32[]{:S(2)}, u32[]{:S(2)}) collective-permute-start(bf16[1280,384]{1,0:T(8,128)(2,1)S(1)} %fusion.16), channel_id=1, source_target_pairs={{0,8},{8,16},{16,24},{24,28},{28,20},{20,12},{12,4},{4,0},{1,9},{9... | collective-permute-start | bytes 2949128 | tf_op jit(solution)/shard_map/ppermute | solution.py:167
  (7 other events, 37.8 us)
Sparse Core Ops, SparseCore 0:
  9.5 217.1 all-gather.2
  486.5 50.4 reduce-scatter.1
